TPU v7x, 256 devices: a whole 4x4x8 slice. The times are simulated.
256 devices in a mesh: blk: 64 (over z, y, x_lo), grp: 4 (over x_hi, core).
Axes of the slice: x: 4 (x_hi: 2, x_lo: 2; x = x_hi * 2 + x_lo), y: 4, z: 8, core: 2. Of those that a mesh axis runs over, the one named last changes fastest.
Arguments:
- features: bfloat16 [196608, 2048], P(('blk', 'grp'))
- factors: bfloat16 [196608, 512], P(('blk', 'grp'))
- pivots: int32 [2, 256], replicated, may hold values from 0 to 767, as said below
- owners: int32 [2], replicated, may hold values from 0 to 255, as said below
Outputs:
- embedding: float32 [196608], P(('blk', 'grp'))
- columns: bfloat16 [196608, 512], P(('blk', 'grp'))
- leftover: float32 [196608], P(('blk', 'grp'))
Inputs may be any that keep to these rules, and one draw needn't show every extreme that they name: `pivots`: each row holds 256 distinct row numbers from 0 to 767. The 2 owners are distinct devices; one of them is the last device.
All inputs are finite; a program needn't handle non-finite values.
Results may differ from a plain program's by a relative error of at most 0.001.
Values may be sent and summed in bfloat16 or wider, within the bound.
No kernel may reach another device: no remote copies, remote signals or barrier semaphores. Data moves between devices by JAX's collectives and lax.ppermute only.
A program may use at most 64 MiB of HBM per device.

v0:
```python
import jax
import jax.numpy as jnp
from jax import lax
from jax.sharding import PartitionSpec as P

F = 2048
ROUNDS = 2


def passed_along(value, axis, steps):
    count = lax.axis_size(axis)
    pairs = [(source, (source + steps) % count) for source in range(count)]
    return lax.ppermute(value, axis, pairs)


def from_root(shard, axis, root):
    mine = lax.axis_index(axis) == root
    return lax.psum(jnp.where(mine, shard, jnp.zeros_like(shard)), axis)


def squares(block):
    wide = block.astype(jnp.float32)
    return jnp.sum(wide * wide, axis=1)


def kernel_block(left, right, left_sq, right_sq):
    gram = jnp.dot(left, right.T, preferred_element_type=jnp.float32)
    dist = left_sq[:, None] + right_sq[None, :] - 2.0 * gram
    return jnp.exp(-dist / (8.0 * F))


def solve_block(piv_x, piv_sq, piv_l):
    schur = kernel_block(piv_x, piv_x, piv_sq, piv_sq) - jnp.dot(
        piv_l, piv_l.T, preferred_element_type=jnp.float32
    )
    lower = jnp.linalg.cholesky(schur)
    ident = jnp.eye(schur.shape[0], dtype=jnp.float32)
    return lax.linalg.triangular_solve(lower, ident, left_side=True, lower=True)


def apply_block(tx, tsq, tl, piv_x, piv_sq, piv_l, inverse):
    cross = kernel_block(tx, piv_x, tsq, piv_sq) - jnp.dot(
        tl, piv_l.T, preferred_element_type=jnp.float32
    )
    return jnp.dot(
        cross, inverse.T, precision=lax.Precision.HIGHEST, preferred_element_type=jnp.float32
    ).astype(jnp.bfloat16)


def on_device(features, factors, pivots, owners):
    rows = features.shape[0]
    own_sq = squares(features)
    grand_total = jnp.sum(kernel_block(features, features, own_sq, own_sq), axis=1)
    carried = features
    for step in range(2):
        carried = passed_along(carried, "blk", 1)
        grand_total = grand_total + jnp.sum(
            kernel_block(features, carried, own_sq, squares(carried)), axis=1
        )
    embedding = grand_total / (3.0 * rows)
    current = factors
    newcols = []
    received = []
    for rnd in range(ROUNDS):
        mine_x = jnp.take(features, pivots[rnd], axis=0)
        mine_l = jnp.take(factors, pivots[rnd], axis=0)
        received.append(
            (
                from_root(mine_x, ("blk", "grp"), owners[rnd]),
                from_root(mine_l, ("blk", "grp"), owners[rnd]),
            )
        )
    blocks_x = []
    block_squared_norms = []
    block_factor_rows = []
    inverses = []
    for rnd in range(ROUNDS):
        piv_x, piv_l = received[rnd]
        piv_sq = squares(piv_x)
        for prior in range(rnd):
            extra = apply_block(
                piv_x,
                piv_sq,
                piv_l,
                blocks_x[prior],
                block_squared_norms[prior],
                block_factor_rows[prior],
                inverses[prior],
            )
            piv_l = jnp.concatenate([piv_l, extra], axis=1)
        inverses.append(solve_block(piv_x, piv_sq, piv_l))
        blocks_x.append(piv_x)
        block_squared_norms.append(piv_sq)
        block_factor_rows.append(piv_l)
    for rnd in range(ROUNDS):
        fresh = apply_block(
            features,
            own_sq,
            current,
            blocks_x[rnd],
            block_squared_norms[rnd],
            block_factor_rows[rnd],
            inverses[rnd],
        )
        newcols.append(fresh)
        current = jnp.concatenate([current, fresh], axis=1)
    columns = jnp.concatenate(newcols, axis=1)
    wide = current.astype(jnp.float32)
    leftover = 1.0 - jnp.sum(wide * wide, axis=1)
    return (embedding, columns, leftover)


def solution(mesh):
    placed = (P(("blk", "grp"), None), P(("blk", "grp"), None), P(), P())
    return jax.shard_map(
        on_device,
        mesh=mesh,
        in_specs=placed,
        out_specs=(P(("blk", "grp")), P(("blk", "grp"), None), P(("blk", "grp"))),
        check_vma=False,
    )
```

profile of v0, /device:TPU:2, one launch (start us, length us, event | category | flops | bytes accessed | tf_op | source)
XLA Modules:
  0.0 551.7 jit_solution(2248281939449981346)
XLA Ops:
  8.1 5.8 %gather_fusion.2 = bf16[256,2048]{1,0:T(8,128)(2,1)} fusion(bf16[768,2048]{1,0:T(8,128)(2,1)} %param.11, s32[1024]{0:T(1024)S(1)} %pad_clamp_fusion), kind=kCustom, calls=%fused_computation.2.clone | custom fusion | bytes 2098176 | tf_op jit(solution)/shard_map/jit(_take)/gather | solution.py:65
  13.9 2.4 gather_fusion
  16.2 3.2 gather_fusion.1
  19.4 2.4 gather_fusion.3
  23.7 2.5 select_select_fusion.1
  26.3 1.8 select_select_fusion.5
  30.0 2.1 collective-permute-start
  34.1 2.8 exponential_reduce_fusion.2
  36.9 283.0 %all-reduce.4.cloned.1.call-done = (bf16[256,2048]{1,0:T(8,128)(2,1)}, bf16[256,2048]{1,0:T(8,128)(2,1)}, bf16[256,512]{1,0:T(8,128)(2,1)}, bf16[256,512]{1,0:T(8,128)(2,1)}) async-done(((bf16[256,2048]{1,0:T(8,128)(2,1)}, bf16[256,2048]{1,0:T(8,128)(2,1)}, bf16[256,512]{1,0:T(8,128)(2,1)}, bf16[256,512]{1,0:T(8,128)(2,1)}), (bf16[256,2048]{1,0:T(8,128)(2,1)}, bf16[256,2048]{1,0:T(8,128)(2,1)}, ...) | async-done | bytes 2621456 | tf_op jit(solution)/shard_map/psum | solution.py:18
  319.9 2.2 multiply_reduce_fusion.4
  322.1 2.0 fusion.25
  327.5 1.8 copy.9
  331.0 11.7 %cholesky.130 = f32[128,128]{1,0:T(8,128)S(1)} custom-call(f32[128,128]{1,0:T(8,128)S(1)} %cholesky.194), custom_call_target="Cholesky" | custom-call | tf_op jit(solution)/shard_map/jit(cholesky)/cholesky | solution.py:36
  344.0 9.8 %custom-call.13 = f32[1,128,128]{1,2,0:T(8,128)S(1)} custom-call(f32[1,128,128]{2,1,0:T(8,128)S(1)} %get-tuple-element.57), custom_call_target="InvertDiagBlocksLowerTriangular" | custom-call | tf_op jit(solution)/shard_map/jit(cholesky)/cholesky | solution.py:36
  353.8 1.7 constant_dynamic-update-slice_fusion.3
  356.6 11.9 %cholesky.147 = f32[128,128]{1,0:T(8,128)S(1)} custom-call(f32[128,128]{1,0:T(8,128)S(1)} %convolution_subtract_fusion.7), custom_call_target="Cholesky" | custom-call | tf_op jit(solution)/shard_map/jit(cholesky)/cholesky | solution.py:36
  368.5 1.3 compare_reduce_fusion.3
  372.4 1.7 select_select_fusion.3
  375.4 7.1 %while.4 = (s32[]{:T(128)}, f32[256,256]{1,0:T(8,128)}, s32[2,2]{1,0:T(2,128)}, f32[2,128,128]{2,1,0:T(8,128)S(1)}, s32[]{:T(128)}) while((s32[]{:T(128)}, f32[256,256]{1,0:T(8,128)}, s32[2,2]{1,0:T(2,128)}, f32[2,128,128]{2,1,0:T(8,128)S(1)}, s32[]{:T(128)}) %tuple.52), condition=%wide.while_cond, body=%wide.while_body.sunk | while | flops 2 | bytes 131189 | solution.py:38
  376.7 2.3 bitcast_dynamic-update-slice_fusion.4
  380.3 2.2 bitcast_dynamic-update-slice_fusion.4
  383.1 20.5 %custom-call.14 = f32[2,128,128]{1,2,0:T(8,128)S(1)} custom-call(f32[2,128,128]{2,1,0:T(8,128)} %copy-done.15), custom_call_target="InvertDiagBlocksLowerTriangular" | custom-call | tf_op jit(solution)/shard_map/triangular_solve/custom-call.0 | solution.py:38
  406.4 1.3 convolution_subtract_fusion.2
  408.9 2.2 convolution_subtract_fusion.1
  411.2 1.8 copy.14
  414.7 11.7 %cholesky.164 = f32[128,128]{1,0:T(8,128)S(1)} custom-call(f32[128,128]{1,0:T(8,128)S(1)} %cholesky.197), custom_call_target="Cholesky" | custom-call | tf_op jit(solution)/shard_map/jit(cholesky)/cholesky | solution.py:36
  427.7 9.8 %custom-call.15 = f32[1,128,128]{1,2,0:T(8,128)S(1)} custom-call(f32[1,128,128]{2,1,0:T(8,128)S(1)} %get-tuple-element.53), custom_call_target="InvertDiagBlocksLowerTriangular" | custom-call | tf_op jit(solution)/shard_map/jit(cholesky)/cholesky | solution.py:36
  437.5 1.7 constant_dynamic-update-slice_fusion.1
  440.3 11.7 %cholesky.181 = f32[128,128]{1,0:T(8,128)S(1)} custom-call(f32[128,128]{1,0:T(8,128)S(1)} %convolution_subtract_fusion.6), custom_call_target="Cholesky" | custom-call | tf_op jit(solution)/shard_map/jit(cholesky)/cholesky | solution.py:36
  455.9 1.7 select_select_fusion.2
  457.6 2.5 fusion.6
  461.5 5.9 %while.5 = (s32[]{:T(128)}, f32[256,256]{1,0:T(8,128)}, s32[2,2]{1,0:T(2,128)S(1)}, f32[2,128,128]{2,1,0:T(8,128)S(1)}, s32[]{:T(128)}) while((s32[]{:T(128)}, f32[256,256]{1,0:T(8,128)}, s32[2,2]{1,0:T(2,128)S(1)}, f32[2,128,128]{2,1,0:T(8,128)S(1)}, s32[]{:T(128)}) %tuple.61), condition=%wide.while_cond.clone, body=%wide.while_body.clone.sunk | while | flops 2 | bytes 131189 | solution.py:38
  462.1 2.3 bitcast_dynamic-update-slice_fusion.5
  465.1 2.3 bitcast_dynamic-update-slice_fusion.5
  468.0 1.5 collective-permute-start.1
  469.5 2.0 convolution_convert_fusion.1
  472.4 21.1 %custom-call.16 = f32[2,128,128]{1,2,0:T(8,128)} custom-call(f32[2,128,128]{2,1,0:T(8,128)} %copy-done.14), custom_call_target="InvertDiagBlocksLowerTriangular" | custom-call | tf_op jit(solution)/shard_map/triangular_solve/custom-call.0 | solution.py:38
  497.2 2.4 fusion.10
  500.1 1.6 convolution_convert_fusion
  501.7 1.9 copy.16
  503.6 1.9 pad_maximum_fusion
  505.6 2.3 copy.17
  507.8 1.7 multiply_reduce_fusion.3
  510.2 2.6 multiply_reduce_fusion.1
  512.8 4.7 exponential_reduce_fusion.1
  517.5 19.1 %collective-permute-done.1 = bf16[768,2048]{1,0:T(8,128)(2,1)} collective-permute-done((bf16[768,2048]{1,0:T(8,128)(2,1)}, bf16[768,2048]{1,0:T(8,128)(2,1)}, u32[]{:S(2)}, u32[]{:S(2)}) %collective-permute-start.1) | collective-permute-done | bytes 3145760 | tf_op jit(solution)/shard_map/ppermute | solution.py:13
  536.6 2.6 multiply_reduce_fusion
  539.1 4.7 exponential_reduce_fusion
  (94 shorter events, 38.7 us)
Async XLA Ops:
  7.2 312.7 %all-reduce.4.cloned.1.call-start = ((), (), s32[]{:S(2)}) async-start(), calls=%async_computation | async-start | bytes 5242880 | tf_op jit(solution)/shard_map/psum | solution.py:18
  8.0 5.8 %copy-start = (bf16[768,2048]{1,0:T(8,128)(2,1)S(1)}, bf16[768,2048]{1,0:T(8,128)(2,1)}, u32[]{:S(2)}) copy-start(bf16[768,2048]{1,0:T(8,128)(2,1)} %param.11) | copy-start | bytes 9437188
  16.2 5.6 %copy-start.16 = (s32[2]{0:T(128)S(1)}, s32[2]{0:T(128)}, u32[]{:S(2)}) copy-start(s32[2]{0:T(128)} %param.14) | copy-start | bytes 28
  23.7 4.3 copy-start.3
  30.0 437.3 %collective-permute-start = (bf16[768,2048]{1,0:T(8,128)(2,1)S(1)}, bf16[768,2048]{1,0:T(8,128)(2,1)}, u32[]{:S(2)}, u32[]{:S(2)}) collective-permute-start(bf16[768,2048]{1,0:T(8,128)(2,1)S(1)} %copy-done), channel_id=1, source_target_pairs={{0,4},{4,8},{8,12},{12,16},{16,20},{20,24},{24,28},{28,32},{32,36}... | collective-permute-start | bytes 9437192 | tf_op jit(solution)/shard_map/ppermute | solution.py:13
  319.9 4.2 copy-start.8
  319.9 4.2 copy-start.9
  324.1 2.4 copy-start.4
  330.3 0.7 copy-start.10
  382.5 0.6 copy-start.15
  404.9 2.9 copy-start.5
  406.4 1.4 copy-start.7
  414.0 0.7 copy-start.11
  457.6 2.6 copy-start.1
  460.1 1.3 copy-start.17
  467.3 0.6 copy-start.14
  468.0 68.6 %collective-permute-start.1 = (bf16[768,2048]{1,0:T(8,128)(2,1)}, bf16[768,2048]{1,0:T(8,128)(2,1)}, u32[]{:S(2)}, u32[]{:S(2)}) collective-permute-start(bf16[768,2048]{1,0:T(8,128)(2,1)} %collective-permute-done), channel_id=1, source_target_pairs={{0,4},{4,8},{8,12},{12,16},{16,20},{20,24},{24,28},{28,32},{32,36}... | collective-permute-start | bytes 9437192 | tf_op jit(solution)/shard_map/ppermute | solution.py:13
  497.1 2.4 copy-start.2
  497.1 2.4 copy-start.6
  497.2 2.4 copy-start.12
  497.2 2.4 copy-start.13
Sparse Core Ops, SparseCore 0:
  30.1 289.7 all-reduce.3
where the time goes:
time: 563 us; the launch traced here: 552 us
  waiting for transfers between devices  302 us (54%)
  other arithmetic  140 us (25%)
  matrix products  43.8 us (8%)
  local copies, waits for them, and re-layouts  42.9 us (8%)
  between operations  18.7 us (3%)
    psum x1, waiting for transfers between devices, from_root(): return lax.psum(jnp.where(mine, shard, jnp.zeros_like(shard)), axis)  283 us
    another operation x14, other arithmetic, solve_block(): lower = jnp.linalg.cholesky(schur)  72.9 us
    another operation x5, other arithmetic, solve_block(): return lax.linalg.triangular_solve(lower, ident, left_side=True, lower=True)  45.6 us
    dot_general x8, matrix products, kernel_block(): gram = jnp.dot(left, right.T, preferred_element_type=jnp.float32)  21.5 us
    ppermute x2, waiting for transfers between devices, passed_along(): return lax.ppermute(value, axis, pairs)  19.1 us
    another operation x15, local copies, waits for them, and re-layouts, solve_block(): return lax.linalg.triangular_solve(lower, ident, left_side=True, lower=True)  14.2 us
  transfers between devices with their start and end apart: 3, of which 2 were waited for; matrix products, arithmetic and copies ran while one was open for 35% of the time, Pallas kernels for 0%

commit v1 on v0

--- a/solution.py
+++ b/solution.py
@@ -13,9 +13,24 @@
     return lax.ppermute(value, axis, pairs)
 
 
-def from_root(shard, axis, root):
-    mine = lax.axis_index(axis) == root
-    return lax.psum(jnp.where(mine, shard, jnp.zeros_like(shard)), axis)
+def device_index():
+    return lax.axis_index("blk") * lax.axis_size("grp") + lax.axis_index("grp")
+
+
+def picked_rows(block, rows, take):
+    selector = (rows[:, None] == jnp.arange(block.shape[0], dtype=rows.dtype)[None, :]) & take
+    return jnp.dot(selector.astype(block.dtype), block, preferred_element_type=jnp.float32)
+
+
+def from_owner(features, factors, rows, owner, after=None):
+    take = device_index() == owner
+    picked = jnp.concatenate(
+        [picked_rows(features, rows, take), picked_rows(factors, rows, take)], axis=1
+    )
+    if after is not None:
+        picked, _ = lax.optimization_barrier((picked, after))
+    wide = lax.psum(picked, ("blk", "grp"))
+    return wide[:, : features.shape[1]], wide[:, features.shape[1] :]
 
 
 def squares(block):
@@ -49,27 +64,20 @@
 
 def on_device(features, factors, pivots, owners):
     rows = features.shape[0]
+    received = []
+    for rnd in range(ROUNDS):
+        after = received[-1][0] if received else None
+        received.append(from_owner(features, factors, pivots[rnd], owners[rnd], after))
     own_sq = squares(features)
     grand_total = jnp.sum(kernel_block(features, features, own_sq, own_sq), axis=1)
-    carried = features
-    for step in range(2):
-        carried = passed_along(carried, "blk", 1)
+    for step in (1, 2):
+        carried = passed_along(features, "blk", step)
         grand_total = grand_total + jnp.sum(
             kernel_block(features, carried, own_sq, squares(carried)), axis=1
         )
     embedding = grand_total / (3.0 * rows)
     current = factors
     newcols = []
-    received = []
-    for rnd in range(ROUNDS):
-        mine_x = jnp.take(features, pivots[rnd], axis=0)
-        mine_l = jnp.take(factors, pivots[rnd], axis=0)
-        received.append(
-            (
-                from_root(mine_x, ("blk", "grp"), owners[rnd]),
-                from_root(mine_l, ("blk", "grp"), owners[rnd]),
-            )
-        )
     blocks_x = []
     block_squared_norms = []
     block_factor_rows = []

time: 563 us -> 644 us (1.14)
  waiting for transfers between devices: 302 us -> 398 us
  local copies, waits for them, and re-layouts: 42.9 us -> 29.5 us
    psum x1, waiting for transfers between devices: 283 us -> 398 us  [from_owner(): wide = lax.psum(picked, ('blk', 'grp'))]
    ppermute x2, waiting for transfers between devices: 19.1 us -> 0.01 us  [passed_along(): return lax.ppermute(value, axis, pairs)]
    gather x4 -> x0, local copies, waits for them, and re-layouts: 13.8 us -> none  [the longest x2 8.17 us: on_device(): mine_x = jnp.take(features, pivots[rnd], axis=0)]
    dot_general x0 -> x4, matrix products: none -> 7.09 us  [picked_rows(): jnp.dot(selector.astype(block.dtype), block, preferred_element_type=jnp.f...]
  transfers between devices with their start and end apart: 3 -> 3, of which waited for: 2 -> 1; matrix products, arithmetic and copies ran while one was open for 35% -> 30% of each run, Pallas kernels for 0% -> 0%
where the time goes in v1:
time: 644 us; the launch traced here: 632 us
  waiting for transfers between devices  398 us (62%)
  other arithmetic  136 us (21%)
  matrix products  46.5 us (7%)
  local copies, waits for them, and re-layouts  29.5 us (5%)
  between operations  18.6 us (3%)
    psum x1, waiting for transfers between devices, from_owner(): wide = lax.psum(picked, ('blk', 'grp'))  398 us
    another operation x14, other arithmetic, solve_block(): lower = jnp.linalg.cholesky(schur)  72.6 us
    another operation x5, other arithmetic, solve_block(): return lax.linalg.triangular_solve(lower, ident, left_side=True, lower=True)  44.2 us
    dot_general x8, matrix products, kernel_block(): gram = jnp.dot(left, right.T, preferred_element_type=jnp.float32)  19.8 us
    another operation x15, local copies, waits for them, and re-layouts, solve_block(): return lax.linalg.triangular_solve(lower, ident, left_side=True, lower=True)  13.8 us
  transfers between devices with their start and end apart: 3, of which 1 were waited for; matrix products, arithmetic and copies ran while one was open for 30% of the time, Pallas kernels for 0%

profile of v1, /device:TPU:2, one launch (start us, length us, event | category | flops | bytes accessed | tf_op | source)
XLA Modules:
  0.0 632.1 jit_solution(2342229118964412712)
XLA Ops:
  7.2 1.3 fusion.122
  10.0 4.4 fusion.76
  14.4 1.2 fusion.74
  18.2 1.8 pad_maximum_fusion.1
  20.0 1.7 pad_maximum_fusion
  21.7 1.6 collective-permute-start
  23.4 1.7 collective-permute-start.1
  26.4 2.8 exponential_reduce_fusion.2
  29.2 398.2 %all-reduce.4.cloned.1.call-done = (f32[256,2560]{1,0:T(8,128)}, f32[256,2560]{1,0:T(8,128)}) async-done(((f32[256,2560]{1,0:T(8,128)}, f32[256,2560]{1,0:T(8,128)}), (f32[256,2560]{1,0:T(8,128)}, f32[256,2560]{1,0:T(8,128)})) %all-reduce.4.cloned.1.call-update) | async-done | bytes 5242896 | tf_op jit(solution)/shard_map/psum | solution.py:32
  427.4 2.7 multiply_reduce_fusion.4
  431.6 1.2 fusion.60
  435.5 1.8 copy.9
  439.1 11.7 %cholesky.130 = f32[128,128]{1,0:T(8,128)S(1)} custom-call(f32[128,128]{1,0:T(8,128)S(1)} %cholesky.194), custom_call_target="Cholesky" | custom-call | tf_op jit(solution)/shard_map/jit(cholesky)/cholesky | solution.py:51
  452.0 9.8 %custom-call.13 = f32[1,128,128]{1,2,0:T(8,128)S(1)} custom-call(f32[1,128,128]{2,1,0:T(8,128)S(1)} %get-tuple-element.55), custom_call_target="InvertDiagBlocksLowerTriangular" | custom-call | tf_op jit(solution)/shard_map/jit(cholesky)/cholesky | solution.py:51
  461.9 1.7 constant_dynamic-update-slice_fusion.3
  464.6 12.1 %cholesky.147 = f32[128,128]{1,0:T(8,128)S(1)} custom-call(f32[128,128]{1,0:T(8,128)S(1)} %convolution_subtract_fusion.7), custom_call_target="Cholesky" | custom-call | tf_op jit(solution)/shard_map/jit(cholesky)/cholesky | solution.py:51
  478.1 1.4 compare_reduce_fusion.3
  480.8 1.7 select_select_fusion.1
  482.5 1.3 broadcast.133
  483.8 7.3 %while.4 = (s32[]{:T(128)}, f32[256,256]{1,0:T(8,128)}, s32[2,2]{1,0:T(2,128)}, f32[2,128,128]{2,1,0:T(8,128)S(1)}, s32[]{:T(128)}) while((s32[]{:T(128)}, f32[256,256]{1,0:T(8,128)}, s32[2,2]{1,0:T(2,128)}, f32[2,128,128]{2,1,0:T(8,128)S(1)}, s32[]{:T(128)}) %tuple.53), condition=%wide.while_cond, body=%wide.while_body.sunk | while | flops 2 | bytes 131181 | solution.py:53
  485.1 2.3 bitcast_dynamic-update-slice_fusion.4
  488.8 2.2 bitcast_dynamic-update-slice_fusion.4
  491.7 20.5 %custom-call.14 = f32[2,128,128]{1,2,0:T(8,128)S(1)} custom-call(f32[2,128,128]{2,1,0:T(8,128)} %copy-done.22), custom_call_target="InvertDiagBlocksLowerTriangular" | custom-call | tf_op jit(solution)/shard_map/triangular_solve/custom-call.0 | solution.py:53
  512.5 1.2 convolution_subtract_fusion.5
  514.6 1.5 fusion.67
  516.8 1.4 convolution_subtract_fusion.1
  520.8 11.7 %cholesky.164 = f32[128,128]{1,0:T(8,128)S(1)} custom-call(f32[128,128]{1,0:T(8,128)S(1)} %cholesky.197), custom_call_target="Cholesky" | custom-call | tf_op jit(solution)/shard_map/jit(cholesky)/cholesky | solution.py:51
  533.1 9.8 %custom-call.15 = f32[1,128,128]{1,2,0:T(8,128)S(1)} custom-call(f32[1,128,128]{2,1,0:T(8,128)S(1)} %get-tuple-element.51), custom_call_target="InvertDiagBlocksLowerTriangular" | custom-call | tf_op jit(solution)/shard_map/jit(cholesky)/cholesky | solution.py:51
  545.0 11.7 %cholesky.181 = f32[128,128]{1,0:T(8,128)S(1)} custom-call(f32[128,128]{1,0:T(8,128)S(1)} %convolution_subtract_fusion.6), custom_call_target="Cholesky" | custom-call | tf_op jit(solution)/shard_map/jit(cholesky)/cholesky | solution.py:51
  557.5 1.2 compare_reduce_fusion.1
  560.9 5.3 while.5
  562.2 1.4 bitcast_dynamic-update-slice_fusion.5
  564.9 1.4 bitcast_dynamic-update-slice_fusion.5
  566.3 20.4 %custom-call.16 = f32[2,128,128]{1,2,0:T(8,128)} custom-call(f32[2,128,128]{2,1,0:T(8,128)S(1)} %get-tuple-element.22), custom_call_target="InvertDiagBlocksLowerTriangular" | custom-call | tf_op jit(solution)/shard_map/triangular_solve/custom-call.0 | solution.py:53
  586.7 2.7 fusion.17
  589.4 1.5 fusion.6
  592.8 1.2 fusion.95
  594.0 1.2 convolution_subtract_fusion.4
  596.5 2.7 fusion.27
  599.8 1.6 convolution_convert_fusion
  601.4 1.9 copy.16
  603.3 1.9 pad_maximum_fusion.3
  605.2 2.3 copy.17
  607.5 1.7 multiply_reduce_fusion.3
  609.9 2.6 multiply_reduce_fusion.1
  612.4 4.7 exponential_reduce_fusion.1
  617.2 2.6 multiply_reduce_fusion
  619.7 4.7 exponential_reduce_fusion
  (96 shorter events, 33.1 us)
Async XLA Ops:
  7.2 420.2 %all-reduce.4.cloned.1.call-start = ((), (), s32[]{:S(2)}) async-start(), calls=%async_computation | async-start | bytes 10485760 | tf_op jit(solution)/shard_map/psum | solution.py:32
  9.9 4.5 copy-start.4
  10.0 6.3 copy-start
  16.3 1.1 copy-start.5
  16.3 1.8 copy-start.3
  16.3 1.9 copy-start.18
  21.7 588.1 %collective-permute-start = (bf16[768,2048]{1,0:T(8,128)(2,1)S(1)}, bf16[768,2048]{1,0:T(8,128)(2,1)}, u32[]{:S(2)}, u32[]{:S(2)}) collective-permute-start(bf16[768,2048]{1,0:T(8,128)(2,1)S(1)} %copy-done), channel_id=1, source_target_pairs={{0,4},{4,8},{8,12},{12,16},{16,20},{20,24},{24,28},{28,32},{32,36}... | collective-permute-start | bytes 9437192 | tf_op jit(solution)/shard_map/ppermute | solution.py:13
  23.4 593.8 %collective-permute-start.1 = (bf16[768,2048]{1,0:T(8,128)(2,1)S(1)}, bf16[768,2048]{1,0:T(8,128)(2,1)}, u32[]{:S(2)}, u32[]{:S(2)}) collective-permute-start(bf16[768,2048]{1,0:T(8,128)(2,1)S(1)} %copy-done), channel_id=1, source_target_pairs={{0,8},{4,12},{8,16},{12,20},{16,24},{20,28},{24,32},{28,36},{32,40... | collective-permute-start | bytes 9437192 | tf_op jit(solution)/shard_map/ppermute | solution.py:13
  25.7 486.8 %copy-start.8 = (f32[256,256]{1,0:T(8,128)}, f32[256,256]{1,0:T(8,128)S(1)}, u32[]{:S(2)}) copy-start(f32[256,256]{1,0:T(8,128)S(1)} %fusion.94) | copy-start | bytes 786436
  427.4 3.0 copy-start.1
  427.4 3.8 copy-start.2
  438.3 0.7 copy-start.16
  491.0 0.6 copy-start.22
  512.5 1.5 copy-start.9
  514.0 0.6 copy-start.13
  516.2 0.6 copy-start.20
  520.1 0.7 copy-start.17
  556.8 3.1 copy-start.15
  566.3 23.2 %copy-start.11 = (f32[256,256]{1,0:T(8,128)}, f32[256,256]{1,0:T(8,128)S(1)}, u32[]{:S(2)}) copy-start(f32[256,256]{1,0:T(8,128)S(1)} %get-tuple-element.166) | copy-start | bytes 786436
  586.7 2.7 copy-start.6
  589.4 1.5 copy-start.10
  589.4 1.5 copy-start.14
  596.4 2.8 copy-start.7
  596.4 2.8 copy-start.12
  596.4 2.8 copy-start.19
  596.4 2.8 copy-start.21
Sparse Core Ops, SparseCore 0:
  21.9 405.4 all-reduce.3

commit v2 on v1

--- a/solution.py
+++ b/solution.py
@@ -22,15 +22,11 @@
     return jnp.dot(selector.astype(block.dtype), block, preferred_element_type=jnp.float32)
 
 
-def from_owner(features, factors, rows, owner, after=None):
+def from_owner(features, factors, rows, owner):
     take = device_index() == owner
-    picked = jnp.concatenate(
+    return jnp.concatenate(
         [picked_rows(features, rows, take), picked_rows(factors, rows, take)], axis=1
     )
-    if after is not None:
-        picked, _ = lax.optimization_barrier((picked, after))
-    wide = lax.psum(picked, ("blk", "grp"))
-    return wide[:, : features.shape[1]], wide[:, features.shape[1] :]
 
 
 def squares(block):
@@ -64,16 +60,19 @@
 
 def on_device(features, factors, pivots, owners):
     rows = features.shape[0]
+    picked = [from_owner(features, factors, pivots[rnd], owners[rnd]) for rnd in range(ROUNDS)]
+    carried = [passed_along(features, "blk", step) for step in (1, 2)]
+    picked, carried = lax.optimization_barrier((picked, carried))
+    width = features.shape[1]
     received = []
     for rnd in range(ROUNDS):
-        after = received[-1][0] if received else None
-        received.append(from_owner(features, factors, pivots[rnd], owners[rnd], after))
+        wide = lax.psum(picked[rnd], ("blk", "grp"))
+        received.append((wide[:, :width], wide[:, width:]))
     own_sq = squares(features)
     grand_total = jnp.sum(kernel_block(features, features, own_sq, own_sq), axis=1)
-    for step in (1, 2):
-        carried = passed_along(features, "blk", step)
+    for other in carried:
         grand_total = grand_total + jnp.sum(
-            kernel_block(features, carried, own_sq, squares(carried)), axis=1
+            kernel_block(features, other, own_sq, squares(other)), axis=1
         )
     embedding = grand_total / (3.0 * rows)
     current = factors

time: 644 us -> 653 us (1.014); the launches traced: 632 us -> 648 us
  waiting for transfers between devices: 398 us -> 444 us
  local copies, waits for them, and re-layouts: 29.5 us -> 12.7 us
  matrix products: 46.5 us -> 35 us
    ppermute x2, waiting for transfers between devices: 0.01 us -> 192 us  [passed_along(): return lax.ppermute(value, axis, pairs)]
    psum x1, waiting for transfers between devices: 398 us -> 253 us  [on_device(): wide = lax.psum(picked[rnd], ('blk', 'grp'))]
    another operation x14, other arithmetic: 72.6 us -> 80.7 us  [solve_block(): lower = jnp.linalg.cholesky(schur)]
  transfers between devices with their start and end apart: 3 -> 3, of which waited for: 1 -> 3; matrix products, arithmetic and copies ran while one was open for 30% -> 5% of each run, Pallas kernels for 0% -> 0%
where the time goes in v2:
time: 653 us; the launch traced here: 648 us
  waiting for transfers between devices  444 us (68%)
  other arithmetic  134 us (21%)
  matrix products  35 us (5%)
  between operations  18.5 us (3%)
  local copies, waits for them, and re-layouts  12.7 us (2%)
    psum x1, waiting for transfers between devices, on_device(): wide = lax.psum(picked[rnd], ('blk', 'grp'))  253 us
    ppermute x2, waiting for transfers between devices, passed_along(): return lax.ppermute(value, axis, pairs)  192 us
    another operation x14, other arithmetic, solve_block(): lower = jnp.linalg.cholesky(schur)  80.7 us
    another operation x5, other arithmetic, solve_block(): return lax.linalg.triangular_solve(lower, ident, left_side=True, lower=True)  39.4 us
    dot_general x8, matrix products, kernel_block(): gram = jnp.dot(left, right.T, preferred_element_type=jnp.float32)  19.5 us
  transfers between devices with their start and end apart: 3, of which 3 were waited for; matrix products, arithmetic and copies ran while one was open for 5% of the time, Pallas kernels for 0%

profile of v2, /device:TPU:2, one launch (start us, length us, event | category | flops | bytes accessed | tf_op | source)
XLA Modules:
  0.0 648.1 jit_solution(11463981807723403786)
XLA Ops:
  7.2 1.6 collective-permute-start
  8.8 1.6 collective-permute-start.1
  10.4 1.3 fusion.166
  13.0 0.8 fusion.165
  13.8 1.7 fusion.116
  15.5 1.6 fusion.121
  17.1 2.6 multiply_reduce_fusion.2
  19.6 1.0 fusion.118
  20.7 1.0 fusion.123
  21.7 2.7 pad_maximum_fusion
  24.4 53.0 %collective-permute-done = bf16[768,2048]{1,0:T(8,128)(2,1)} collective-permute-done((bf16[768,2048]{1,0:T(8,128)(2,1)}, bf16[768,2048]{1,0:T(8,128)(2,1)}, u32[]{:S(2)}, u32[]{:S(2)}) %collective-permute-start) | collective-permute-done | bytes 3145760 | tf_op jit(solution)/shard_map/ppermute | solution.py:13
  77.4 138.8 %collective-permute-done.1 = bf16[768,2048]{1,0:T(8,128)(2,1)} collective-permute-done((bf16[768,2048]{1,0:T(8,128)(2,1)}, bf16[768,2048]{1,0:T(8,128)(2,1)}, u32[]{:S(2)}, u32[]{:S(2)}) %collective-permute-start.1) | collective-permute-done | bytes 3145760 | tf_op jit(solution)/shard_map/ppermute | solution.py:13
  216.2 2.8 exponential_reduce_fusion
  219.1 2.6 multiply_reduce_fusion
  221.7 2.6 multiply_reduce_fusion.1
  224.2 4.8 fusion.3
  229.0 4.8 fusion.7
  234.4 252.5 %all-reduce.4.cloned.1.call-done = (f32[256,2560]{1,0:T(8,128)}, f32[256,2560]{1,0:T(8,128)}) async-done(((f32[256,2560]{1,0:T(8,128)}, f32[256,2560]{1,0:T(8,128)}), (f32[256,2560]{1,0:T(8,128)}, f32[256,2560]{1,0:T(8,128)})) %all-reduce.4.cloned.1.call-update) | async-done | bytes 5242896 | tf_op jit(solution)/shard_map/psum | solution.py:69
  486.9 1.8 multiply_reduce_fusion.5
  488.8 3.0 fusion.53
  492.6 1.9 fusion.41
  495.0 0.7 slice.106
  495.7 1.2 fusion.111
  497.8 11.7 %cholesky.130 = f32[128,128]{1,0:T(8,128)S(1)} custom-call(f32[128,128]{1,0:T(8,128)S(1)} %cholesky.194), custom_call_target="Cholesky" | custom-call | tf_op jit(solution)/shard_map/jit(cholesky)/cholesky | solution.py:47
  509.6 9.8 %custom-call.13 = f32[1,128,128]{1,2,0:T(8,128)S(1)} custom-call(f32[1,128,128]{2,1,0:T(8,128)S(1)} %get-tuple-element.61), custom_call_target="InvertDiagBlocksLowerTriangular" | custom-call | tf_op jit(solution)/shard_map/jit(cholesky)/cholesky | solution.py:47
  519.9 22.9 %cholesky.147 = f32[128,128]{1,0:T(8,128)S(1)} custom-call(f32[128,128]{1,0:T(8,128)S(1)} %convolution_subtract_fusion.7), custom_call_target="Cholesky" | custom-call | tf_op jit(solution)/shard_map/jit(cholesky)/cholesky | solution.py:47
  542.7 0.7 compare_reduce_fusion.3
  543.4 0.7 compare_reduce_fusion.2
  545.5 4.0 while.4
  546.2 1.4 bitcast_dynamic-update-slice_fusion.4
  548.2 1.4 bitcast_dynamic-update-slice_fusion.4
  549.6 19.7 %custom-call.14 = f32[2,128,128]{1,2,0:T(8,128)S(1)} custom-call(f32[2,128,128]{2,1,0:T(8,128)S(1)} %get-tuple-element.27), custom_call_target="InvertDiagBlocksLowerTriangular" | custom-call | tf_op jit(solution)/shard_map/triangular_solve/custom-call.0 | solution.py:49
  570.2 0.8 convolution_convert_fusion.1
  571.2 1.5 convolution_subtract_fusion.2
  573.3 1.4 convolution_subtract_fusion.1
  574.9 11.7 %cholesky.164 = f32[128,128]{1,0:T(8,128)S(1)} custom-call(f32[128,128]{1,0:T(8,128)S(1)} %cholesky.197), custom_call_target="Cholesky" | custom-call | tf_op jit(solution)/shard_map/jit(cholesky)/cholesky | solution.py:47
  586.7 9.8 %custom-call.15 = f32[1,128,128]{1,2,0:T(8,128)S(1)} custom-call(f32[1,128,128]{2,1,0:T(8,128)S(1)} %get-tuple-element.57), custom_call_target="InvertDiagBlocksLowerTriangular" | custom-call | tf_op jit(solution)/shard_map/jit(cholesky)/cholesky | solution.py:47
  597.0 11.9 %cholesky.181 = f32[128,128]{1,0:T(8,128)S(1)} custom-call(f32[128,128]{1,0:T(8,128)S(1)} %convolution_subtract_fusion.6), custom_call_target="Cholesky" | custom-call | tf_op jit(solution)/shard_map/jit(cholesky)/cholesky | solution.py:47
  608.8 0.7 compare_reduce_fusion.1
  609.6 0.7 compare_reduce_fusion
  611.6 4.0 while.5
  611.6 0.6 fusion.194
  612.2 1.3 bitcast_dynamic-update-slice_fusion.5
  614.3 1.3 bitcast_dynamic-update-slice_fusion.5
  615.6 19.7 %custom-call.16 = f32[2,128,128]{1,2,0:T(8,128)S(1)} custom-call(f32[2,128,128]{2,1,0:T(8,128)S(1)} %get-tuple-element.28), custom_call_target="InvertDiagBlocksLowerTriangular" | custom-call | tf_op jit(solution)/shard_map/triangular_solve/custom-call.0 | solution.py:49
  636.2 1.6 convolution_subtract_fusion
  637.8 0.8 convolution_convert_fusion
  638.9 1.2 copy.18
  (60 shorter events, 9.8 us)
Async XLA Ops:
  7.2 479.8 %all-reduce.4.cloned.1.call-start = ((), (), s32[]{:S(2)}) async-start(), calls=%async_computation | async-start | bytes 10485760 | tf_op jit(solution)/shard_map/psum | solution.py:69
  7.2 70.2 %collective-permute-start = (bf16[768,2048]{1,0:T(8,128)(2,1)}, bf16[768,2048]{1,0:T(8,128)(2,1)}, u32[]{:S(2)}, u32[]{:S(2)}) collective-permute-start(bf16[768,2048]{1,0:T(8,128)(2,1)} %param.7), channel_id=1, source_target_pairs={{0,4},{4,8},{8,12},{12,16},{16,20},{20,24},{24,28},{28,32},{32,36}... | collective-permute-start | bytes 9437192 | tf_op jit(solution)/shard_map/ppermute | solution.py:13
  8.8 207.4 %collective-permute-start.1 = (bf16[768,2048]{1,0:T(8,128)(2,1)}, bf16[768,2048]{1,0:T(8,128)(2,1)}, u32[]{:S(2)}, u32[]{:S(2)}) collective-permute-start(bf16[768,2048]{1,0:T(8,128)(2,1)} %param.7), channel_id=1, source_target_pairs={{0,8},{4,12},{8,16},{12,20},{16,24},{20,28},{24,32},{28,36},{32,40... | collective-permute-start | bytes 9437192 | tf_op jit(solution)/shard_map/ppermute | solution.py:13
  13.8 5.8 copy-start
  488.8 3.1 copy-start.1
  488.8 3.6 copy-start.2
  494.5 2.4 copy-start.3
  574.7 61.5 %copy-start.4 = (bf16[256,512]{1,0:T(8,128)(2,1)S(1)}, bf16[256,512]{1,0:T(8,128)(2,1)}, u32[]{:S(2)}) copy-start(bf16[256,512]{1,0:T(8,128)(2,1)} %slice.106) | copy-start | bytes 786436
Sparse Core Ops, SparseCore 0:
  216.4 270.5 all-reduce.3

commit v3 on v2

--- a/solution.py
+++ b/solution.py
@@ -26,7 +26,37 @@
     take = device_index() == owner
     return jnp.concatenate(
         [picked_rows(features, rows, take), picked_rows(factors, rows, take)], axis=1
-    )
+    ).astype(jnp.bfloat16)
+
+
+def flip_pairs(bit, count):
+    return [(source, source ^ (1 << bit)) for source in range(count)]
+
+
+def broadcast_sum(value, order):
+    axes = ("blk", "grp")
+    count = lax.axis_size(axes)
+    me = device_index()
+    current = value
+    for bit in order:
+        half = current.shape[0] // 2
+        upper = ((me >> bit) & 1) == 1
+        keep = jnp.where(upper, current[half:], current[:half])
+        send = jnp.where(upper, current[:half], current[half:])
+        current = keep + lax.ppermute(send, axes, flip_pairs(bit, count))
+    for bit in reversed(order):
+        upper = ((me >> bit) & 1) == 1
+        other = lax.ppermute(current, axes, flip_pairs(bit, count))
+        current = jnp.where(
+            upper, jnp.concatenate([other, current]), jnp.concatenate([current, other])
+        )
+    return current
+
+
+def bit_order(count):
+    bits = count.bit_length() - 1
+    near = [0, 2, 3, 5, 1, 4, 6, 7]
+    return [b for b in near if b < bits] + list(range(len(near), bits))
 
 
 def squares(block):
@@ -60,14 +90,15 @@
 
 def on_device(features, factors, pivots, owners):
     rows = features.shape[0]
-    picked = [from_owner(features, factors, pivots[rnd], owners[rnd]) for rnd in range(ROUNDS)]
-    carried = [passed_along(features, "blk", step) for step in (1, 2)]
-    picked, carried = lax.optimization_barrier((picked, carried))
+    count = lax.axis_size(("blk", "grp"))
     width = features.shape[1]
     received = []
     for rnd in range(ROUNDS):
-        wide = lax.psum(picked[rnd], ("blk", "grp"))
+        picked = from_owner(features, factors, pivots[rnd], owners[rnd])
+        wide = broadcast_sum(picked, bit_order(count))
         received.append((wide[:, :width], wide[:, width:]))
+    shifted, _ = lax.optimization_barrier((features, received[-1][0]))
+    carried = [passed_along(shifted, "blk", step) for step in (1, 2)]
     own_sq = squares(features)
     grand_total = jnp.sum(kernel_block(features, features, own_sq, own_sq), axis=1)
     for other in carried:

time: 653 us -> 480 us (0.74)
  waiting for transfers between devices: 444 us -> 77.5 us
  starting transfers between devices: 3.24 us -> 175 us
  local copies, waits for them, and re-layouts: 12.7 us -> 26.7 us
  between operations: 18.5 us -> 5.26 us
  matrix products: 35 us -> 47.2 us
  other arithmetic: 134 us -> 141 us
    psum x1 -> x0, waiting for transfers between devices: 253 us -> none  [on_device(): wide = lax.psum(picked[rnd], ('blk', 'grp'))]
    ppermute x2, waiting for transfers between devices: 192 us -> 0.01 us  [passed_along(): return lax.ppermute(value, axis, pairs)]
    ppermute x0 -> x32, starting transfers between devices: none -> 172 us  [the longest x16 138 us: broadcast_sum(): other = lax.ppermute(current, axes, flip_pairs(bit, count))]
    ppermute x0 -> x32, waiting for transfers between devices: none -> 77.5 us  [the longest x16 62.1 us: broadcast_sum(): current = keep + lax.ppermute(send, axes, flip_pairs(bit, count))]
    another operation x14 -> x13, other arithmetic: 80.7 us -> 78 us  [solve_block(): lower = jnp.linalg.cholesky(schur)]
  transfers between devices with their start and end apart: 3 -> 34, of which waited for: 3 -> 14; matrix products, arithmetic and copies ran while one was open for 5% -> 43% of each run, Pallas kernels for 0% -> 0%
where the time goes in v3:
time: 480 us; the launch traced here: 473 us
  starting transfers between devices  175 us (36%)
  other arithmetic  141 us (29%)
  waiting for transfers between devices  77.5 us (16%)
  matrix products  47.2 us (10%)
  local copies, waits for them, and re-layouts  26.7 us (6%)
  between operations  5.26 us (1%)
    ppermute x16, starting transfers between devices, broadcast_sum(): other = lax.ppermute(current, axes, flip_pairs(bit, count))  138 us
    another operation x13, other arithmetic, solve_block(): lower = jnp.linalg.cholesky(schur)  78 us
    ppermute x16, waiting for transfers between devices, broadcast_sum(): current = keep + lax.ppermute(send, axes, flip_pairs(bit, count))  62.1 us
    another operation x5, other arithmetic, solve_block(): return lax.linalg.triangular_solve(lower, ident, left_side=True, lower=True)  43.2 us
    ppermute x16, starting transfers between devices, broadcast_sum(): current = keep + lax.ppermute(send, axes, flip_pairs(bit, count))  34.1 us
    dot_general x8, matrix products, kernel_block(): gram = jnp.dot(left, right.T, preferred_element_type=jnp.float32)  20 us
    ppermute x16, waiting for transfers between devices, broadcast_sum(): other = lax.ppermute(current, axes, flip_pairs(bit, count))  15.4 us
    another operation x15, local copies, waits for them, and re-layouts, solve_block(): return lax.linalg.triangular_solve(lower, ident, left_side=True, lower=True)  13.8 us
  transfers between devices with their start and end apart: 34, of which 14 were waited for; matrix products, arithmetic and copies ran while one was open for 43% of the time, Pallas kernels for 0%

profile of v3, /device:TPU:2, one launch (start us, length us, event | category | flops | bytes accessed | tf_op | source)
XLA Modules:
  0.0 473.2 jit_solution(12407282615884500402)
XLA Ops:
  6.6 3.0 convolution_convert_fusion.1
  11.6 2.9 convolution_convert_fusion
  16.5 2.6 multiply_reduce_fusion.2
  24.1 55.1 %collective-permute-done.1 = bf16[64,2560]{1,0:T(8,128)(2,1)S(1)} collective-permute-done((bf16[64,2560]{1,0:T(8,128)(2,1)S(1)}, bf16[64,2560]{1,0:T(8,128)(2,1)S(1)}, u32[]{:S(2)}, u32[]{:S(2)}) %collective-permute-start.1) | collective-permute-done | bytes 327712 | tf_op jit(solution)/shard_map/ppermute | solution.py:46
  80.7 4.2 collective-permute-done.19
  86.6 2.0 collective-permute-start.3
  90.4 2.0 collective-permute-start.21
  92.4 2.2 collective-permute-start.4
  94.9 2.2 collective-permute-start.22
  98.0 3.3 collective-permute-start.5
  101.4 2.7 collective-permute-start.23
  104.2 3.4 collective-permute-start.6
  107.6 2.8 collective-permute-start.24
  110.5 5.7 %collective-permute-start.7 = (bf16[1,2560]{1,0:T(2,128)(2,1)S(1)}, bf16[1,2560]{1,0:T(2,128)(2,1)S(1)}, u32[]{:S(2)}, u32[]{:S(2)}) collective-permute-start(bf16[1,2560]{1,0:T(2,128)(2,1)S(1)} %broadcast_select_fusion.18), channel_id=1, source_target_pairs={{0,128},{1,129},{2,130},{3,131},{4,132},{5,133},{6,134},{7,135},{8... | collective-permute-start | bytes 15368 | tf_op jit(solution)/shard_map/ppermute | solution.py:46
  116.2 2.0 collective-permute-start.25
  118.3 5.6 %collective-permute-start.8 = (bf16[1,2560]{1,0:T(2,128)(2,1)S(1)}, bf16[1,2560]{1,0:T(2,128)(2,1)S(1)}, u32[]{:S(2)}, u32[]{:S(2)}) collective-permute-start(bf16[1,2560]{1,0:T(2,128)(2,1)S(1)} %fusion.56), channel_id=1, source_target_pairs={{0,128},{1,129},{2,130},{3,131},{4,132},{5,133},{6,134},{7,135},{8... | collective-permute-start | bytes 15368 | tf_op jit(solution)/shard_map/ppermute | solution.py:49
  123.9 2.0 collective-permute-start.26
  127.7 3.9 collective-permute-done.26
  133.3 2.3 collective-permute-start.10
  136.4 2.3 collective-permute-start.28
  138.7 2.3 collective-permute-start.11
  141.9 2.2 collective-permute-start.29
  148.9 101.6 %collective-permute-start.13 = (bf16[32,2560]{1,0:T(8,128)(2,1)S(1)}, bf16[32,2560]{1,0:T(8,128)(2,1)S(1)}, u32[]{:S(2)}, u32[]{:S(2)}) collective-permute-start(bf16[32,2560]{1,0:T(8,128)(2,1)S(1)} %maximum_select_fusion.6), channel_id=1, source_target_pairs={{0,8},{1,9},{2,10},{3,11},{4,12},{5,13},{6,14},{7,15},{8,0},{9,1},... | collective-permute-start | bytes 491528 | tf_op jit(solution)/shard_map/ppermute | solution.py:49
  250.5 2.4 collective-permute-start.31
  254.0 2.3 collective-permute-done.31
  256.4 4.6 collective-permute-done.14
  261.1 10.7 %collective-permute-start.15 = (bf16[128,2560]{1,0:T(8,128)(2,1)S(1)}, bf16[128,2560]{1,0:T(8,128)(2,1)S(1)}, u32[]{:S(2)}, u32[]{:S(2)}) collective-permute-start(bf16[128,2560]{1,0:T(8,128)(2,1)S(1)} %maximum_select_fusion.2), channel_id=1, source_target_pairs={{0,1},{1,0},{2,3},{3,2},{4,5},{5,4},{6,7},{7,6},{8,9},{9,8},{10,11... | collective-permute-start | bytes 1966088 | tf_op jit(solution)/shard_map/ppermute | solution.py:49
  271.8 2.8 exponential_reduce_fusion
  288.4 11.7 %cholesky.130 = f32[128,128]{1,0:T(8,128)S(1)} custom-call(f32[128,128]{1,0:T(8,128)S(1)} %cholesky.194), custom_call_target="Cholesky" | custom-call | tf_op jit(solution)/shard_map/jit(cholesky)/cholesky | solution.py:77
  300.8 9.8 %custom-call.13 = f32[1,128,128]{1,2,0:T(8,128)S(1)} custom-call(f32[1,128,128]{2,1,0:T(8,128)S(1)} %get-tuple-element.53), custom_call_target="InvertDiagBlocksLowerTriangular" | custom-call | tf_op jit(solution)/shard_map/jit(cholesky)/cholesky | solution.py:77
  313.5 12.1 %cholesky.147 = f32[128,128]{1,0:T(8,128)S(1)} custom-call(f32[128,128]{1,0:T(8,128)S(1)} %convolution_subtract_fusion.7), custom_call_target="Cholesky" | custom-call | tf_op jit(solution)/shard_map/jit(cholesky)/cholesky | solution.py:77
  331.1 7.3 %while.4 = (s32[]{:T(128)}, f32[256,256]{1,0:T(8,128)}, s32[2,2]{1,0:T(2,128)}, f32[2,128,128]{2,1,0:T(8,128)S(1)}, s32[]{:T(128)}) while((s32[]{:T(128)}, f32[256,256]{1,0:T(8,128)}, s32[2,2]{1,0:T(2,128)}, f32[2,128,128]{2,1,0:T(8,128)S(1)}, s32[]{:T(128)}) %tuple.53), condition=%wide.while_cond, body=%wide.while_body.sunk | while | flops 2 | bytes 131181 | solution.py:79
  332.5 2.3 bitcast_dynamic-update-slice_fusion.4
  336.1 2.2 bitcast_dynamic-update-slice_fusion.4
  338.4 20.3 %custom-call.14 = f32[2,128,128]{1,2,0:T(8,128)} custom-call(f32[2,128,128]{2,1,0:T(8,128)S(1)} %get-tuple-element.21), custom_call_target="InvertDiagBlocksLowerTriangular" | custom-call | tf_op jit(solution)/shard_map/triangular_solve/custom-call.0 | solution.py:79
  370.1 13.2 %cholesky.164 = f32[128,128]{1,0:T(8,128)} custom-call(f32[128,128]{1,0:T(8,128)} %cholesky.197), custom_call_target="Cholesky" | custom-call | tf_op jit(solution)/shard_map/jit(cholesky)/cholesky | solution.py:77
  383.3 2.0 select_reduce_fusion.1
  386.8 11.3 %custom-call.15 = f32[1,128,128]{1,2,0:T(8,128)} custom-call(f32[1,128,128]{2,1,0:T(8,128)} %get-tuple-element.49), custom_call_target="InvertDiagBlocksLowerTriangular" | custom-call | tf_op jit(solution)/shard_map/jit(cholesky)/cholesky | solution.py:77
  401.5 13.2 %cholesky.181 = f32[128,128]{1,0:T(8,128)} custom-call(f32[128,128]{1,0:T(8,128)} %convolution_subtract_fusion.6), custom_call_target="Cholesky" | custom-call | tf_op jit(solution)/shard_map/jit(cholesky)/cholesky | solution.py:77
  418.1 2.6 fusion.8
  423.0 5.3 %while.5 = (s32[]{:T(128)}, f32[256,256]{1,0:T(8,128)S(1)}, s32[2,2]{1,0:T(2,128)}, f32[2,128,128]{2,1,0:T(8,128)S(1)}, s32[]{:T(128)}) while((s32[]{:T(128)}, f32[256,256]{1,0:T(8,128)S(1)}, s32[2,2]{1,0:T(2,128)}, f32[2,128,128]{2,1,0:T(8,128)S(1)}, s32[]{:T(128)}) %tuple.59), condition=%wide.while_cond.clone, body=%wide.while_body.clone.sunk | while | flops 2 | bytes 131181 | solution.py:79
  428.3 2.0 convolution_convert_fusion.3
  430.3 19.7 %custom-call.16 = f32[2,128,128]{1,2,0:T(8,128)S(1)} custom-call(f32[2,128,128]{2,1,0:T(8,128)S(1)} %get-tuple-element.22), custom_call_target="InvertDiagBlocksLowerTriangular" | custom-call | tf_op jit(solution)/shard_map/triangular_solve/custom-call.0 | solution.py:79
  451.1 3.0 fusion.9
  457.8 2.6 multiply_reduce_fusion.1
  460.4 4.7 fusion.7
  465.1 2.6 multiply_reduce_fusion
  467.7 4.7 fusion.3
  (185 shorter events, 87.0 us)
Async XLA Ops:
  0.6 457.2 %collective-permute-start.16 = (bf16[768,2048]{1,0:T(8,128)(2,1)}, bf16[768,2048]{1,0:T(8,128)(2,1)}, u32[]{:S(2)}, u32[]{:S(2)}) collective-permute-start(bf16[768,2048]{1,0:T(8,128)(2,1)} %param.7), channel_id=1, source_target_pairs={{0,4},{4,8},{8,12},{12,16},{16,20},{20,24},{24,28},{28,32},{32,36}... | collective-permute-start | bytes 9437192 | tf_op jit(solution)/shard_map/ppermute | solution.py:13
  2.3 462.9 %collective-permute-start.17 = (bf16[768,2048]{1,0:T(8,128)(2,1)}, bf16[768,2048]{1,0:T(8,128)(2,1)}, u32[]{:S(2)}, u32[]{:S(2)}) collective-permute-start(bf16[768,2048]{1,0:T(8,128)(2,1)} %param.7), channel_id=1, source_target_pairs={{0,8},{4,12},{8,16},{12,20},{16,24},{20,28},{24,32},{28,36},{32,40... | collective-permute-start | bytes 9437192 | tf_op jit(solution)/shard_map/ppermute | solution.py:13
  6.6 3.0 copy-start.3
  11.0 8.1 %collective-permute-start = (bf16[128,2560]{1,0:T(8,128)(2,1)}, bf16[128,2560]{1,0:T(8,128)(2,1)}, u32[]{:S(2)}, u32[]{:S(2)}) collective-permute-start(bf16[128,2560]{1,0:T(8,128)(2,1)} %broadcast_select_fusion.1), channel_id=1, source_target_pairs={{0,1},{1,0},{2,3},{3,2},{4,5},{5,4},{6,7},{7,6},{8,9},{9,8},{10,11... | collective-permute-start | bytes 1966088 | tf_op jit(solution)/shard_map/ppermute | solution.py:46
  16.0 5.0 %collective-permute-start.18 = (bf16[128,2560]{1,0:T(8,128)(2,1)}, bf16[128,2560]{1,0:T(8,128)(2,1)}, u32[]{:S(2)}, u32[]{:S(2)}) collective-permute-start(bf16[128,2560]{1,0:T(8,128)(2,1)} %broadcast_select_fusion), channel_id=1, source_target_pairs={{0,1},{1,0},{2,3},{3,2},{4,5},{5,4},{6,7},{7,6},{8,9},{9,8},{10,11... | collective-permute-start | bytes 1966088 | tf_op jit(solution)/shard_map/ppermute | solution.py:46
  20.5 58.7 %collective-permute-start.1 = (bf16[64,2560]{1,0:T(8,128)(2,1)S(1)}, bf16[64,2560]{1,0:T(8,128)(2,1)S(1)}, u32[]{:S(2)}, u32[]{:S(2)}) collective-permute-start(bf16[64,2560]{1,0:T(8,128)(2,1)S(1)} %broadcast_select_fusion.3), channel_id=1, source_target_pairs={{0,4},{1,5},{2,6},{3,7},{4,0},{5,1},{6,2},{7,3},{8,12},{9,13},{10,... | collective-permute-start | bytes 983048 | tf_op jit(solution)/shard_map/ppermute | solution.py:46
  22.4 62.4 %collective-permute-start.19 = (bf16[64,2560]{1,0:T(8,128)(2,1)S(1)}, bf16[64,2560]{1,0:T(8,128)(2,1)S(1)}, u32[]{:S(2)}, u32[]{:S(2)}) collective-permute-start(bf16[64,2560]{1,0:T(8,128)(2,1)S(1)} %broadcast_select_fusion.2), channel_id=1, source_target_pairs={{0,4},{1,5},{2,6},{3,7},{4,0},{5,1},{6,2},{7,3},{8,12},{9,13},{10,... | collective-permute-start | bytes 983048 | tf_op jit(solution)/shard_map/ppermute | solution.py:46
  79.2 7.4 %collective-permute-start.2 = (bf16[32,2560]{1,0:T(8,128)(2,1)S(1)}, bf16[32,2560]{1,0:T(8,128)(2,1)S(1)}, u32[]{:S(2)}, u32[]{:S(2)}) collective-permute-start(bf16[32,2560]{1,0:T(8,128)(2,1)S(1)} %broadcast_select_fusion.5), channel_id=1, source_target_pairs={{0,8},{1,9},{2,10},{3,11},{4,12},{5,13},{6,14},{7,15},{8,0},{9,1},... | collective-permute-start | bytes 491528 | tf_op jit(solution)/shard_map/ppermute | solution.py:46
  84.9 5.4 %collective-permute-start.20 = (bf16[32,2560]{1,0:T(8,128)(2,1)S(1)}, bf16[32,2560]{1,0:T(8,128)(2,1)S(1)}, u32[]{:S(2)}, u32[]{:S(2)}) collective-permute-start(bf16[32,2560]{1,0:T(8,128)(2,1)S(1)} %broadcast_select_fusion.4), channel_id=1, source_target_pairs={{0,8},{1,9},{2,10},{3,11},{4,12},{5,13},{6,14},{7,15},{8,0},{9,1},... | collective-permute-start | bytes 491528 | tf_op jit(solution)/shard_map/ppermute | solution.py:46
  86.6 5.7 %collective-permute-start.3 = (bf16[16,2560]{1,0:T(8,128)(2,1)S(1)}, bf16[16,2560]{1,0:T(8,128)(2,1)S(1)}, u32[]{:S(2)}, u32[]{:S(2)}) collective-permute-start(bf16[16,2560]{1,0:T(8,128)(2,1)S(1)} %broadcast_select_fusion.7), channel_id=1, source_target_pairs={{0,32},{1,33},{2,34},{3,35},{4,36},{5,37},{6,38},{7,39},{8,40},{9,... | collective-permute-start | bytes 245768 | tf_op jit(solution)/shard_map/ppermute | solution.py:46
  90.4 4.5 collective-permute-start.21
  92.4 5.6 %collective-permute-start.4 = (bf16[8,2560]{1,0:T(8,128)(2,1)S(1)}, bf16[8,2560]{1,0:T(8,128)(2,1)S(1)}, u32[]{:S(2)}, u32[]{:S(2)}) collective-permute-start(bf16[8,2560]{1,0:T(8,128)(2,1)S(1)} %broadcast_select_fusion.9), channel_id=1, source_target_pairs={{0,2},{1,3},{2,0},{3,1},{4,6},{5,7},{6,4},{7,5},{8,10},{9,11},{10,... | collective-permute-start | bytes 122888 | tf_op jit(solution)/shard_map/ppermute | solution.py:46
  94.9 6.4 %collective-permute-start.22 = (bf16[8,2560]{1,0:T(8,128)(2,1)S(1)}, bf16[8,2560]{1,0:T(8,128)(2,1)S(1)}, u32[]{:S(2)}, u32[]{:S(2)}) collective-permute-start(bf16[8,2560]{1,0:T(8,128)(2,1)S(1)} %broadcast_select_fusion.8), channel_id=1, source_target_pairs={{0,2},{1,3},{2,0},{3,1},{4,6},{5,7},{6,4},{7,5},{8,10},{9,11},{10,... | collective-permute-start | bytes 122888 | tf_op jit(solution)/shard_map/ppermute | solution.py:46
  98.0 6.1 %collective-permute-start.5 = (bf16[4,2560]{1,0:T(4,128)(2,1)S(1)}, bf16[4,2560]{1,0:T(4,128)(2,1)S(1)}, u32[]{:S(2)}, u32[]{:S(2)}) collective-permute-start(bf16[4,2560]{1,0:T(4,128)(2,1)S(1)} %broadcast_select_fusion.11), channel_id=1, source_target_pairs={{0,16},{1,17},{2,18},{3,19},{4,20},{5,21},{6,22},{7,23},{8,24},{9,... | collective-permute-start | bytes 61448 | tf_op jit(solution)/shard_map/ppermute | solution.py:46
  101.4 6.2 %collective-permute-start.23 = (bf16[4,2560]{1,0:T(4,128)(2,1)S(1)}, bf16[4,2560]{1,0:T(4,128)(2,1)S(1)}, u32[]{:S(2)}, u32[]{:S(2)}) collective-permute-start(bf16[4,2560]{1,0:T(4,128)(2,1)S(1)} %broadcast_select_fusion.10), channel_id=1, source_target_pairs={{0,16},{1,17},{2,18},{3,19},{4,20},{5,21},{6,22},{7,23},{8,24},{9,... | collective-permute-start | bytes 61448 | tf_op jit(solution)/shard_map/ppermute | solution.py:46
  104.2 6.3 %collective-permute-start.6 = (bf16[2,2560]{1,0:T(2,128)(2,1)S(1)}, bf16[2,2560]{1,0:T(2,128)(2,1)S(1)}, u32[]{:S(2)}, u32[]{:S(2)}) collective-permute-start(bf16[2,2560]{1,0:T(2,128)(2,1)S(1)} %broadcast_select_fusion.14), channel_id=1, source_target_pairs={{0,64},{1,65},{2,66},{3,67},{4,68},{5,69},{6,70},{7,71},{8,72},{9,... | collective-permute-start | bytes 30728 | tf_op jit(solution)/shard_map/ppermute | solution.py:46
  107.6 164.3 %copy-start = (bf16[768,2048]{1,0:T(8,128)(2,1)S(1)}, bf16[768,2048]{1,0:T(8,128)(2,1)}, u32[]{:S(2)}) copy-start(bf16[768,2048]{1,0:T(8,128)(2,1)} %param.7) | copy-start | bytes 9437188
  107.6 8.6 %collective-permute-start.24 = (bf16[2,2560]{1,0:T(2,128)(2,1)S(1)}, bf16[2,2560]{1,0:T(2,128)(2,1)S(1)}, u32[]{:S(2)}, u32[]{:S(2)}) collective-permute-start(bf16[2,2560]{1,0:T(2,128)(2,1)S(1)} %broadcast_select_fusion.12), channel_id=1, source_target_pairs={{0,64},{1,65},{2,66},{3,67},{4,68},{5,69},{6,70},{7,71},{8,72},{9,... | collective-permute-start | bytes 30728 | tf_op jit(solution)/shard_map/ppermute | solution.py:46
  110.5 7.8 %collective-permute-start.7 = (bf16[1,2560]{1,0:T(2,128)(2,1)S(1)}, bf16[1,2560]{1,0:T(2,128)(2,1)S(1)}, u32[]{:S(2)}, u32[]{:S(2)}) collective-permute-start(bf16[1,2560]{1,0:T(2,128)(2,1)S(1)} %broadcast_select_fusion.18), channel_id=1, source_target_pairs={{0,128},{1,129},{2,130},{3,131},{4,132},{5,133},{6,134},{7,135},{8... | collective-permute-start | bytes 15368 | tf_op jit(solution)/shard_map/ppermute | solution.py:46
  116.2 7.7 %collective-permute-start.25 = (bf16[1,2560]{1,0:T(2,128)(2,1)S(1)}, bf16[1,2560]{1,0:T(2,128)(2,1)S(1)}, u32[]{:S(2)}, u32[]{:S(2)}) collective-permute-start(bf16[1,2560]{1,0:T(2,128)(2,1)S(1)} %broadcast_select_fusion.16), channel_id=1, source_target_pairs={{0,128},{1,129},{2,130},{3,131},{4,132},{5,133},{6,134},{7,135},{8... | collective-permute-start | bytes 15368 | tf_op jit(solution)/shard_map/ppermute | solution.py:46
  118.3 7.7 %collective-permute-start.8 = (bf16[1,2560]{1,0:T(2,128)(2,1)S(1)}, bf16[1,2560]{1,0:T(2,128)(2,1)S(1)}, u32[]{:S(2)}, u32[]{:S(2)}) collective-permute-start(bf16[1,2560]{1,0:T(2,128)(2,1)S(1)} %fusion.56), channel_id=1, source_target_pairs={{0,128},{1,129},{2,130},{3,131},{4,132},{5,133},{6,134},{7,135},{8... | collective-permute-start | bytes 15368 | tf_op jit(solution)/shard_map/ppermute | solution.py:49
  123.9 7.7 %collective-permute-start.26 = (bf16[1,2560]{1,0:T(2,128)(2,1)S(1)}, bf16[1,2560]{1,0:T(2,128)(2,1)S(1)}, u32[]{:S(2)}, u32[]{:S(2)}) collective-permute-start(bf16[1,2560]{1,0:T(2,128)(2,1)S(1)} %fusion.57), channel_id=1, source_target_pairs={{0,128},{1,129},{2,130},{3,131},{4,132},{5,133},{6,134},{7,135},{8... | collective-permute-start | bytes 15368 | tf_op jit(solution)/shard_map/ppermute | solution.py:49
  126.0 7.2 %collective-permute-start.9 = (bf16[2,2560]{1,0:T(2,128)(2,1)S(1)}, bf16[2,2560]{1,0:T(2,128)(2,1)S(1)}, u32[]{:S(2)}, u32[]{:S(2)}) collective-permute-start(bf16[2,2560]{1,0:T(2,128)(2,1)S(1)} %broadcast_select_fusion.21), channel_id=1, source_target_pairs={{0,64},{1,65},{2,66},{3,67},{4,68},{5,69},{6,70},{7,71},{8,72},{9,... | collective-permute-start | bytes 30728 | tf_op jit(solution)/shard_map/ppermute | solution.py:49
  131.6 4.7 collective-permute-start.27
  133.3 5.4 %collective-permute-start.10 = (bf16[4,2560]{1,0:T(4,128)(2,1)S(1)}, bf16[4,2560]{1,0:T(4,128)(2,1)S(1)}, u32[]{:S(2)}, u32[]{:S(2)}) collective-permute-start(bf16[4,2560]{1,0:T(4,128)(2,1)S(1)} %maximum_select_fusion.12), channel_id=1, source_target_pairs={{0,16},{1,17},{2,18},{3,19},{4,20},{5,21},{6,22},{7,23},{8,24},{9,... | collective-permute-start | bytes 61448 | tf_op jit(solution)/shard_map/ppermute | solution.py:49
  136.4 5.5 %collective-permute-start.28 = (bf16[4,2560]{1,0:T(4,128)(2,1)S(1)}, bf16[4,2560]{1,0:T(4,128)(2,1)S(1)}, u32[]{:S(2)}, u32[]{:S(2)}) collective-permute-start(bf16[4,2560]{1,0:T(4,128)(2,1)S(1)} %maximum_select_fusion.13), channel_id=1, source_target_pairs={{0,16},{1,17},{2,18},{3,19},{4,20},{5,21},{6,22},{7,23},{8,24},{9,... | collective-permute-start | bytes 61448 | tf_op jit(solution)/shard_map/ppermute | solution.py:49
  138.7 5.6 %collective-permute-start.11 = (bf16[8,2560]{1,0:T(8,128)(2,1)S(1)}, bf16[8,2560]{1,0:T(8,128)(2,1)S(1)}, u32[]{:S(2)}, u32[]{:S(2)}) collective-permute-start(bf16[8,2560]{1,0:T(8,128)(2,1)S(1)} %maximum_select_fusion.10), channel_id=1, source_target_pairs={{0,2},{1,3},{2,0},{3,1},{4,6},{5,7},{6,4},{7,5},{8,10},{9,11},{10,... | collective-permute-start | bytes 122888 | tf_op jit(solution)/shard_map/ppermute | solution.py:49
  141.9 5.6 %collective-permute-start.29 = (bf16[8,2560]{1,0:T(8,128)(2,1)S(1)}, bf16[8,2560]{1,0:T(8,128)(2,1)S(1)}, u32[]{:S(2)}, u32[]{:S(2)}) collective-permute-start(bf16[8,2560]{1,0:T(8,128)(2,1)S(1)} %maximum_select_fusion.11), channel_id=1, source_target_pairs={{0,2},{1,3},{2,0},{3,1},{4,6},{5,7},{6,4},{7,5},{8,10},{9,11},{10,... | collective-permute-start | bytes 122888 | tf_op jit(solution)/shard_map/ppermute | solution.py:49
  144.3 4.5 collective-permute-start.12
  147.5 103.0 %collective-permute-start.30 = (bf16[16,2560]{1,0:T(8,128)(2,1)S(1)}, bf16[16,2560]{1,0:T(8,128)(2,1)S(1)}, u32[]{:S(2)}, u32[]{:S(2)}) collective-permute-start(bf16[16,2560]{1,0:T(8,128)(2,1)S(1)} %maximum_select_fusion.9), channel_id=1, source_target_pairs={{0,32},{1,33},{2,34},{3,35},{4,36},{5,37},{6,38},{7,39},{8,40},{9,... | collective-permute-start | bytes 245768 | tf_op jit(solution)/shard_map/ppermute | solution.py:49
  148.9 104.9 %collective-permute-start.13 = (bf16[32,2560]{1,0:T(8,128)(2,1)S(1)}, bf16[32,2560]{1,0:T(8,128)(2,1)S(1)}, u32[]{:S(2)}, u32[]{:S(2)}) collective-permute-start(bf16[32,2560]{1,0:T(8,128)(2,1)S(1)} %maximum_select_fusion.6), channel_id=1, source_target_pairs={{0,8},{1,9},{2,10},{3,11},{4,12},{5,13},{6,14},{7,15},{8,0},{9,1},... | collective-permute-start | bytes 491528 | tf_op jit(solution)/shard_map/ppermute | solution.py:49
  250.5 5.7 %collective-permute-start.31 = (bf16[32,2560]{1,0:T(8,128)(2,1)S(1)}, bf16[32,2560]{1,0:T(8,128)(2,1)S(1)}, u32[]{:S(2)}, u32[]{:S(2)}) collective-permute-start(bf16[32,2560]{1,0:T(8,128)(2,1)S(1)} %maximum_select_fusion.7), channel_id=1, source_target_pairs={{0,8},{1,9},{2,10},{3,11},{4,12},{5,13},{6,14},{7,15},{8,0},{9,1},... | collective-permute-start | bytes 491528 | tf_op jit(solution)/shard_map/ppermute | solution.py:49
  253.9 7.2 %collective-permute-start.14 = (bf16[64,2560]{1,0:T(8,128)(2,1)S(1)}, bf16[64,2560]{1,0:T(8,128)(2,1)S(1)}, u32[]{:S(2)}, u32[]{:S(2)}) collective-permute-start(bf16[64,2560]{1,0:T(8,128)(2,1)S(1)} %maximum_select_fusion.4), channel_id=1, source_target_pairs={{0,4},{1,5},{2,6},{3,7},{4,0},{5,1},{6,2},{7,3},{8,12},{9,13},{10,... | collective-permute-start | bytes 983048 | tf_op jit(solution)/shard_map/ppermute | solution.py:49
  256.3 19.1 %collective-permute-start.32 = (bf16[64,2560]{1,0:T(8,128)(2,1)S(1)}, bf16[64,2560]{1,0:T(8,128)(2,1)S(1)}, u32[]{:S(2)}, u32[]{:S(2)}) collective-permute-start(bf16[64,2560]{1,0:T(8,128)(2,1)S(1)} %maximum_select_fusion.5), channel_id=1, source_target_pairs={{0,4},{1,5},{2,6},{3,7},{4,0},{5,1},{6,2},{7,3},{8,12},{9,13},{10,... | collective-permute-start | bytes 983048 | tf_op jit(solution)/shard_map/ppermute | solution.py:49
  261.1 15.5 %collective-permute-start.15 = (bf16[128,2560]{1,0:T(8,128)(2,1)S(1)}, bf16[128,2560]{1,0:T(8,128)(2,1)S(1)}, u32[]{:S(2)}, u32[]{:S(2)}) collective-permute-start(bf16[128,2560]{1,0:T(8,128)(2,1)S(1)} %maximum_select_fusion.2), channel_id=1, source_target_pairs={{0,1},{1,0},{2,3},{3,2},{4,5},{5,4},{6,7},{7,6},{8,9},{9,8},{10,11... | collective-permute-start | bytes 1966088 | tf_op jit(solution)/shard_map/ppermute | solution.py:49
  275.5 2.3 collective-permute-start.33
  279.5 2.4 copy-start.1
  287.7 0.7 copy-start.6
  328.1 36.8 %copy-start.12 = (f32[256]{0:T(256)S(1)}, f32[256]{0:T(256)}, u32[]{:S(2)}) copy-start(f32[256]{0:T(256)} %multiply_reduce_fusion.4) | copy-start | bytes 3076
  358.7 6.2 %copy-start.8 = (bf16[256,512]{1,0:T(8,128)(2,1)S(1)}, bf16[256,512]{1,0:T(8,128)(2,1)}, u32[]{:S(2)}) copy-start(bf16[256,512]{1,0:T(8,128)(2,1)} %slice.298) | copy-start | bytes 786436
  358.7 6.2 %copy-start.13 = (f32[256,256]{0,1:T(8,128)S(1)}, f32[256,256]{0,1:T(8,128)}, u32[]{:S(2)}) copy-start(f32[256,256]{0,1:T(8,128)} %convolution_multiply_fusion.2) | copy-start | bytes 786436
  362.4 1.3 copy-start.5
  364.3 0.7 copy-start.10
  368.8 0.7 copy-start.7
  420.7 29.4 %copy-start.4 = (f32[256,256]{1,0:T(8,128)S(1)}, f32[256,256]{1,0:T(8,128)}, u32[]{:S(2)}) copy-start(f32[256,256]{1,0:T(8,128)} %fusion.38) | copy-start | bytes 786436
  451.0 3.0 copy-start.9
  451.1 3.0 copy-start.11
  456.8 3.6 copy-start.2

commit v4 on v3

--- a/solution.py
+++ b/solution.py
@@ -95,6 +95,9 @@
     received = []
     for rnd in range(ROUNDS):
         picked = from_owner(features, factors, pivots[rnd], owners[rnd])
+        if received:
+            picked, earlier = lax.optimization_barrier((picked, received[-1]))
+            received[-1] = earlier
         wide = broadcast_sum(picked, bit_order(count))
         received.append((wide[:, :width], wide[:, width:]))
     shifted, _ = lax.optimization_barrier((features, received[-1][0]))

time: 480 us -> 488 us (1.017)
  the two profiles are of different devices: /device:TPU:2 before, /device:TPU:55 now
where the time goes in v4:
time: 488 us; the launch traced here: 479 us
  starting transfers between devices  185 us (38%)
  other arithmetic  127 us (26%)
  waiting for transfers between devices  110 us (23%)
  matrix products  36.9 us (8%)
  local copies, waits for them, and re-layouts  14 us (3%)
  between operations  5.88 us (1%)
    ppermute x16, starting transfers between devices, broadcast_sum(): other = lax.ppermute(current, axes, flip_pairs(bit, count))  158 us
    ppermute x16, waiting for transfers between devices, broadcast_sum(): other = lax.ppermute(current, axes, flip_pairs(bit, count))  74.9 us
    another operation x13, other arithmetic, solve_block(): lower = jnp.linalg.cholesky(schur)  68.8 us
    another operation x5, other arithmetic, solve_block(): return lax.linalg.triangular_solve(lower, ident, left_side=True, lower=True)  40.8 us
    ppermute x16, waiting for transfers between devices, broadcast_sum(): current = keep + lax.ppermute(send, axes, flip_pairs(bit, count))  35.2 us
    ppermute x16, starting transfers between devices, broadcast_sum(): current = keep + lax.ppermute(send, axes, flip_pairs(bit, count))  22.5 us
    dot_general x8, matrix products, kernel_block(): gram = jnp.dot(left, right.T, preferred_element_type=jnp.float32)  19.2 us
  transfers between devices with their start and end apart: 34, of which 22 were waited for; matrix products, arithmetic and copies ran while one was open for 21% of the time, Pallas kernels for 0%

profile of v4, /device:TPU:55, one launch (start us, length us, event | category | flops | bytes accessed | tf_op | source)
XLA Modules:
  0.0 478.9 jit_solution(6570840525303485090)
XLA Ops:
  3.4 3.0 convolution_convert_fusion
  10.4 8.3 %collective-permute-done.1 = bf16[64,2560]{1,0:T(8,128)(2,1)S(1)} collective-permute-done((bf16[64,2560]{1,0:T(8,128)(2,1)S(1)}, bf16[64,2560]{1,0:T(8,128)(2,1)S(1)}, u32[]{:S(2)}, u32[]{:S(2)}) %collective-permute-start.1) | collective-permute-done | bytes 327712 | tf_op jit(solution)/shard_map/ppermute | solution.py:46
  19.9 3.5 collective-permute-done.2
  23.6 3.3 collective-permute-done.3
  28.1 3.2 collective-permute-done.4
  31.5 4.1 collective-permute-done.5
  35.7 3.1 collective-permute-start.6
  39.9 5.5 %collective-permute-start.7 = (bf16[1,2560]{1,0:T(2,128)(2,1)S(1)}, bf16[1,2560]{1,0:T(2,128)(2,1)S(1)}, u32[]{:S(2)}, u32[]{:S(2)}) collective-permute-start(bf16[1,2560]{1,0:T(2,128)(2,1)S(1)} %broadcast_select_fusion.18), channel_id=1, source_target_pairs={{0,128},{1,129},{2,130},{3,131},{4,132},{5,133},{6,134},{7,135},{8... | collective-permute-start | bytes 15368 | tf_op jit(solution)/shard_map/ppermute | solution.py:46
  46.4 5.5 %collective-permute-start.8 = (bf16[1,2560]{1,0:T(2,128)(2,1)S(1)}, bf16[1,2560]{1,0:T(2,128)(2,1)S(1)}, u32[]{:S(2)}, u32[]{:S(2)}) collective-permute-start(bf16[1,2560]{1,0:T(2,128)(2,1)S(1)} %fusion.57), channel_id=1, source_target_pairs={{0,128},{1,129},{2,130},{3,131},{4,132},{5,133},{6,134},{7,135},{8... | collective-permute-start | bytes 15368 | tf_op jit(solution)/shard_map/ppermute | solution.py:49
  53.0 2.4 collective-permute-start.9
  56.7 2.2 collective-permute-start.32
  58.9 2.8 collective-permute-start.33
  63.3 2.9 convolution_convert_fusion.1
  66.2 52.4 %collective-permute-done.11 = bf16[8,2560]{1,0:T(8,128)(2,1)S(1)} collective-permute-done((bf16[8,2560]{1,0:T(8,128)(2,1)S(1)}, bf16[8,2560]{1,0:T(8,128)(2,1)S(1)}, u32[]{:S(2)}, u32[]{:S(2)}) %collective-permute-start.11) | collective-permute-done | bytes 40992 | tf_op jit(solution)/shard_map/ppermute | solution.py:49
  120.0 2.4 collective-permute-done.12
  122.5 118.5 %collective-permute-start.13 = (bf16[32,2560]{1,0:T(8,128)(2,1)S(1)}, bf16[32,2560]{1,0:T(8,128)(2,1)S(1)}, u32[]{:S(2)}, u32[]{:S(2)}) collective-permute-start(bf16[32,2560]{1,0:T(8,128)(2,1)S(1)} %maximum_select_fusion.6), channel_id=1, source_target_pairs={{0,8},{1,9},{2,10},{3,11},{4,12},{5,13},{6,14},{7,15},{8,0},{9,1},... | collective-permute-start | bytes 491528 | tf_op jit(solution)/shard_map/ppermute | solution.py:49
  241.1 2.6 collective-permute-done.13
  244.4 2.7 multiply_reduce_fusion.2
  247.1 2.9 collective-permute-done.14
  250.1 9.2 %collective-permute-start.15 = (bf16[128,2560]{1,0:T(8,128)(2,1)S(1)}, bf16[128,2560]{1,0:T(8,128)(2,1)S(1)}, u32[]{:S(2)}, u32[]{:S(2)}) collective-permute-start(bf16[128,2560]{1,0:T(8,128)(2,1)S(1)} %maximum_select_fusion.2), channel_id=1, source_target_pairs={{0,1},{1,0},{2,3},{3,2},{4,5},{5,4},{6,7},{7,6},{8,9},{9,8},{10,11... | collective-permute-start | bytes 1966088 | tf_op jit(solution)/shard_map/ppermute | solution.py:49
  259.3 3.4 exponential_reduce_fusion
  266.1 11.7 %cholesky.130 = f32[128,128]{1,0:T(8,128)S(1)} custom-call(f32[128,128]{1,0:T(8,128)S(1)} %cholesky.194), custom_call_target="Cholesky" | custom-call | tf_op jit(solution)/shard_map/jit(cholesky)/cholesky | solution.py:77
  280.3 9.8 %custom-call.13 = f32[1,128,128]{1,2,0:T(8,128)S(1)} custom-call(f32[1,128,128]{2,1,0:T(8,128)S(1)} %get-tuple-element.59), custom_call_target="InvertDiagBlocksLowerTriangular" | custom-call | tf_op jit(solution)/shard_map/jit(cholesky)/cholesky | solution.py:77
  291.9 1.8 collective-permute-start.18
  294.8 11.7 %cholesky.147 = f32[128,128]{1,0:T(8,128)S(1)} custom-call(f32[128,128]{1,0:T(8,128)S(1)} %convolution_subtract_fusion.7), custom_call_target="Cholesky" | custom-call | tf_op jit(solution)/shard_map/jit(cholesky)/cholesky | solution.py:77
  306.8 3.2 collective-permute-done.19
  314.7 4.1 collective-permute-done.21
  318.8 2.3 collective-permute-start.22
  321.2 3.9 while.4
  325.9 4.3 collective-permute-start.23
  330.2 2.9 fusion.14
  333.1 3.7 collective-permute-start.24
  337.3 20.5 %custom-call.14 = f32[2,128,128]{1,2,0:T(8,128)S(1)} custom-call(f32[2,128,128]{2,1,0:T(8,128)} %copy-done.13), custom_call_target="InvertDiagBlocksLowerTriangular" | custom-call | tf_op jit(solution)/shard_map/triangular_solve/custom-call.0 | solution.py:79
  360.3 1.8 collective-permute-done.25
  362.6 3.9 collective-permute-done.26
  368.3 2.6 collective-permute-done.27
  372.6 2.6 collective-permute-done.28
  376.3 2.6 multiply_reduce_fusion.1
  382.1 4.7 fusion.7
  386.8 2.6 multiply_reduce_fusion
  389.5 12.5 %collective-permute-start.31 = (bf16[128,2560]{1,0:T(8,128)(2,1)S(1)}, bf16[128,2560]{1,0:T(8,128)(2,1)S(1)}, u32[]{:S(2)}, u32[]{:S(2)}) collective-permute-start(bf16[128,2560]{1,0:T(8,128)(2,1)S(1)} %maximum_select_fusion.3), channel_id=1, source_target_pairs={{0,1},{1,0},{2,3},{3,2},{4,5},{5,4},{6,7},{7,6},{8,9},{9,8},{10,11... | collective-permute-start | bytes 1966088 | tf_op jit(solution)/shard_map/ppermute | solution.py:49
  402.1 4.7 fusion.3
  409.0 1.9 fusion.9
  412.3 11.7 %cholesky.164 = f32[128,128]{1,0:T(8,128)S(1)} custom-call(f32[128,128]{1,0:T(8,128)S(1)} %cholesky.197), custom_call_target="Cholesky" | custom-call | tf_op jit(solution)/shard_map/jit(cholesky)/cholesky | solution.py:77
  424.1 9.8 %custom-call.15 = f32[1,128,128]{1,2,0:T(8,128)S(1)} custom-call(f32[1,128,128]{2,1,0:T(8,128)S(1)} %get-tuple-element.55), custom_call_target="InvertDiagBlocksLowerTriangular" | custom-call | tf_op jit(solution)/shard_map/jit(cholesky)/cholesky | solution.py:77
  434.4 11.9 %cholesky.181 = f32[128,128]{1,0:T(8,128)S(1)} custom-call(f32[128,128]{1,0:T(8,128)S(1)} %convolution_subtract_fusion.6), custom_call_target="Cholesky" | custom-call | tf_op jit(solution)/shard_map/jit(cholesky)/cholesky | solution.py:77
  449.0 4.0 while.5
  453.0 19.7 %custom-call.16 = f32[2,128,128]{1,2,0:T(8,128)S(1)} custom-call(f32[2,128,128]{2,1,0:T(8,128)S(1)} %get-tuple-element.28), custom_call_target="InvertDiagBlocksLowerTriangular" | custom-call | tf_op jit(solution)/shard_map/triangular_solve/custom-call.0 | solution.py:79
  (200 shorter events, 59.9 us)
Async XLA Ops:
  3.4 3.0 copy-start.2
  7.0 2.5 collective-permute-start
  9.8 9.0 %collective-permute-start.1 = (bf16[64,2560]{1,0:T(8,128)(2,1)S(1)}, bf16[64,2560]{1,0:T(8,128)(2,1)S(1)}, u32[]{:S(2)}, u32[]{:S(2)}) collective-permute-start(bf16[64,2560]{1,0:T(8,128)(2,1)S(1)} %broadcast_select_fusion.3), channel_id=1, source_target_pairs={{0,4},{1,5},{2,6},{3,7},{4,0},{5,1},{6,2},{7,3},{8,12},{9,13},{10,... | collective-permute-start | bytes 983048 | tf_op jit(solution)/shard_map/ppermute | solution.py:46
  18.8 4.6 collective-permute-start.2
  23.5 3.4 collective-permute-start.3
  26.9 4.4 collective-permute-start.4
  31.4 4.2 collective-permute-start.5
  35.7 4.1 collective-permute-start.6
  39.9 6.5 %collective-permute-start.7 = (bf16[1,2560]{1,0:T(2,128)(2,1)S(1)}, bf16[1,2560]{1,0:T(2,128)(2,1)S(1)}, u32[]{:S(2)}, u32[]{:S(2)}) collective-permute-start(bf16[1,2560]{1,0:T(2,128)(2,1)S(1)} %broadcast_select_fusion.18), channel_id=1, source_target_pairs={{0,128},{1,129},{2,130},{3,131},{4,132},{5,133},{6,134},{7,135},{8... | collective-permute-start | bytes 15368 | tf_op jit(solution)/shard_map/ppermute | solution.py:46
  46.4 6.5 %collective-permute-start.8 = (bf16[1,2560]{1,0:T(2,128)(2,1)S(1)}, bf16[1,2560]{1,0:T(2,128)(2,1)S(1)}, u32[]{:S(2)}, u32[]{:S(2)}) collective-permute-start(bf16[1,2560]{1,0:T(2,128)(2,1)S(1)} %fusion.57), channel_id=1, source_target_pairs={{0,128},{1,129},{2,130},{3,131},{4,132},{5,133},{6,134},{7,135},{8... | collective-permute-start | bytes 15368 | tf_op jit(solution)/shard_map/ppermute | solution.py:49
  53.0 3.5 collective-permute-start.9
  56.6 5.8 %collective-permute-start.10 = (bf16[4,2560]{1,0:T(4,128)(2,1)S(1)}, bf16[4,2560]{1,0:T(4,128)(2,1)S(1)}, u32[]{:S(2)}, u32[]{:S(2)}) collective-permute-start(bf16[4,2560]{1,0:T(4,128)(2,1)S(1)} %maximum_select_fusion.12), channel_id=1, source_target_pairs={{0,16},{1,17},{2,18},{3,19},{4,20},{5,21},{6,22},{7,23},{8,24},{9,... | collective-permute-start | bytes 61448 | tf_op jit(solution)/shard_map/ppermute | solution.py:49
  56.7 319.6 %collective-permute-start.32 = (bf16[768,2048]{1,0:T(8,128)(2,1)}, bf16[768,2048]{1,0:T(8,128)(2,1)}, u32[]{:S(2)}, u32[]{:S(2)}) collective-permute-start(bf16[768,2048]{1,0:T(8,128)(2,1)} %param.7), channel_id=1, source_target_pairs={{0,4},{4,8},{8,12},{12,16},{16,20},{20,24},{24,28},{28,32},{32,36}... | collective-permute-start | bytes 9437192 | tf_op jit(solution)/shard_map/ppermute | solution.py:13
  58.9 327.9 %collective-permute-start.33 = (bf16[768,2048]{1,0:T(8,128)(2,1)}, bf16[768,2048]{1,0:T(8,128)(2,1)}, u32[]{:S(2)}, u32[]{:S(2)}) collective-permute-start(bf16[768,2048]{1,0:T(8,128)(2,1)} %param.7), channel_id=1, source_target_pairs={{0,8},{4,12},{8,16},{12,20},{16,24},{20,28},{24,32},{28,36},{32,40... | collective-permute-start | bytes 9437192 | tf_op jit(solution)/shard_map/ppermute | solution.py:13
  62.4 56.3 %collective-permute-start.11 = (bf16[8,2560]{1,0:T(8,128)(2,1)S(1)}, bf16[8,2560]{1,0:T(8,128)(2,1)S(1)}, u32[]{:S(2)}, u32[]{:S(2)}) collective-permute-start(bf16[8,2560]{1,0:T(8,128)(2,1)S(1)} %maximum_select_fusion.10), channel_id=1, source_target_pairs={{0,2},{1,3},{2,0},{3,1},{4,6},{5,7},{6,4},{7,5},{8,10},{9,11},{10,... | collective-permute-start | bytes 122888 | tf_op jit(solution)/shard_map/ppermute | solution.py:49
  118.7 3.8 collective-permute-start.12
  122.5 121.2 %collective-permute-start.13 = (bf16[32,2560]{1,0:T(8,128)(2,1)S(1)}, bf16[32,2560]{1,0:T(8,128)(2,1)S(1)}, u32[]{:S(2)}, u32[]{:S(2)}) collective-permute-start(bf16[32,2560]{1,0:T(8,128)(2,1)S(1)} %maximum_select_fusion.6), channel_id=1, source_target_pairs={{0,8},{1,9},{2,10},{3,11},{4,12},{5,13},{6,14},{7,15},{8,0},{9,1},... | collective-permute-start | bytes 491528 | tf_op jit(solution)/shard_map/ppermute | solution.py:49
  243.7 6.3 %collective-permute-start.14 = (bf16[64,2560]{1,0:T(8,128)(2,1)S(1)}, bf16[64,2560]{1,0:T(8,128)(2,1)S(1)}, u32[]{:S(2)}, u32[]{:S(2)}) collective-permute-start(bf16[64,2560]{1,0:T(8,128)(2,1)S(1)} %maximum_select_fusion.4), channel_id=1, source_target_pairs={{0,4},{1,5},{2,6},{3,7},{4,0},{5,1},{6,2},{7,3},{8,12},{9,13},{10,... | collective-permute-start | bytes 983048 | tf_op jit(solution)/shard_map/ppermute | solution.py:49
  244.4 15.0 %copy-start = (bf16[768,2048]{1,0:T(8,128)(2,1)S(1)}, bf16[768,2048]{1,0:T(8,128)(2,1)}, u32[]{:S(2)}) copy-start(bf16[768,2048]{1,0:T(8,128)(2,1)} %param.7) | copy-start | bytes 9437188
  250.1 12.6 %collective-permute-start.15 = (bf16[128,2560]{1,0:T(8,128)(2,1)S(1)}, bf16[128,2560]{1,0:T(8,128)(2,1)S(1)}, u32[]{:S(2)}, u32[]{:S(2)}) collective-permute-start(bf16[128,2560]{1,0:T(8,128)(2,1)S(1)} %maximum_select_fusion.2), channel_id=1, source_target_pairs={{0,1},{1,0},{2,3},{3,2},{4,5},{5,4},{6,7},{7,6},{8,9},{9,8},{10,11... | collective-permute-start | bytes 1966088 | tf_op jit(solution)/shard_map/ppermute | solution.py:49
  264.1 14.4 %collective-permute-start.16 = (bf16[128,2560]{1,0:T(8,128)(2,1)}, bf16[128,2560]{1,0:T(8,128)(2,1)}, u32[]{:S(2)}, u32[]{:S(2)}) collective-permute-start(bf16[128,2560]{1,0:T(8,128)(2,1)} %broadcast_select_fusion), channel_id=1, source_target_pairs={{0,1},{1,0},{2,3},{3,2},{4,5},{5,4},{6,7},{7,6},{8,9},{9,8},{10,11... | collective-permute-start | bytes 1966088 | tf_op jit(solution)/shard_map/ppermute | solution.py:46
  264.4 65.8 %copy-start.15 = (f32[256]{0:T(256)}, f32[256]{0:T(256)S(1)}, u32[]{:S(2)}) copy-start(f32[256]{0:T(256)S(1)} %multiply_reduce_fusion.5) | copy-start | bytes 3076
  279.8 12.1 %collective-permute-start.17 = (bf16[64,2560]{1,0:T(8,128)(2,1)S(1)}, bf16[64,2560]{1,0:T(8,128)(2,1)S(1)}, u32[]{:S(2)}, u32[]{:S(2)}) collective-permute-start(bf16[64,2560]{1,0:T(8,128)(2,1)S(1)} %broadcast_select_fusion.2), channel_id=1, source_target_pairs={{0,4},{1,5},{2,6},{3,7},{4,0},{5,1},{6,2},{7,3},{8,12},{9,13},{10,... | collective-permute-start | bytes 983048 | tf_op jit(solution)/shard_map/ppermute | solution.py:46
  280.3 40.8 %copy-start.19 = (s32[2]{0:T(128)S(1)}, s32[2]{0:T(128)}, u32[]{:S(2)}) copy-start(s32[2]{0:T(128)} %iota_multiply_fusion) | copy-start | bytes 28
  291.8 14.9 %copy-start.8 = (f32[256,256]{1,0:T(8,128)S(1)}, f32[256,256]{1,0:T(8,128)}, u32[]{:S(2)}) copy-start(f32[256,256]{1,0:T(8,128)} %get-tuple-element.64) | copy-start | bytes 786436
  291.9 14.6 %collective-permute-start.18 = (bf16[32,2560]{1,0:T(8,128)(2,1)S(1)}, bf16[32,2560]{1,0:T(8,128)(2,1)S(1)}, u32[]{:S(2)}, u32[]{:S(2)}) collective-permute-start(bf16[32,2560]{1,0:T(8,128)(2,1)S(1)} %broadcast_select_fusion.4), channel_id=1, source_target_pairs={{0,8},{1,9},{2,10},{3,11},{4,12},{5,13},{6,14},{7,15},{8,0},{9,1},... | collective-permute-start | bytes 491528 | tf_op jit(solution)/shard_map/ppermute | solution.py:46
  306.6 3.4 collective-permute-start.19
  310.0 4.4 collective-permute-start.20
  314.5 4.2 collective-permute-start.21
  318.8 6.4 %collective-permute-start.22 = (bf16[2,2560]{1,0:T(2,128)(2,1)S(1)}, bf16[2,2560]{1,0:T(2,128)(2,1)S(1)}, u32[]{:S(2)}, u32[]{:S(2)}) collective-permute-start(bf16[2,2560]{1,0:T(2,128)(2,1)S(1)} %broadcast_select_fusion.12), channel_id=1, source_target_pairs={{0,64},{1,65},{2,66},{3,67},{4,68},{5,69},{6,70},{7,71},{8,72},{9,... | collective-permute-start | bytes 30728 | tf_op jit(solution)/shard_map/ppermute | solution.py:46
  325.2 7.9 %copy-start.17 = (s32[2,2]{1,0:T(2,128)}, s32[2,2]{1,0:T(2,128)S(1)}, u32[]{:S(2)}) copy-start(s32[2,2]{1,0:T(2,128)S(1)} %get-tuple-element.221) | copy-start | bytes 52
  325.8 11.0 %copy-start.3 = (bf16[768,512]{1,0:T(8,128)(2,1)S(1)}, bf16[768,512]{1,0:T(8,128)(2,1)}, u32[]{:S(2)}) copy-start(bf16[768,512]{1,0:T(8,128)(2,1)} %param.8) | copy-start | bytes 2359300
  325.9 7.2 %collective-permute-start.23 = (bf16[1,2560]{1,0:T(2,128)(2,1)S(1)}, bf16[1,2560]{1,0:T(2,128)(2,1)S(1)}, u32[]{:S(2)}, u32[]{:S(2)}) collective-permute-start(bf16[1,2560]{1,0:T(2,128)(2,1)S(1)} %broadcast_select_fusion.16), channel_id=1, source_target_pairs={{0,128},{1,129},{2,130},{3,131},{4,132},{5,133},{6,134},{7,135},{8... | collective-permute-start | bytes 15368 | tf_op jit(solution)/shard_map/ppermute | solution.py:46
  333.1 24.7 %collective-permute-start.24 = (bf16[1,2560]{1,0:T(2,128)(2,1)S(1)}, bf16[1,2560]{1,0:T(2,128)(2,1)}, u32[]{:S(2)}, u32[]{:S(2)}) collective-permute-start(bf16[1,2560]{1,0:T(2,128)(2,1)S(1)} %fusion.58), channel_id=1, source_target_pairs={{0,128},{1,129},{2,130},{3,131},{4,132},{5,133},{6,134},{7,135},{8... | collective-permute-start | bytes 15368 | tf_op jit(solution)/shard_map/ppermute | solution.py:49
  357.8 4.4 copy-start.12
  358.6 3.5 collective-permute-start.25
  360.3 11.3 %copy-start.4 = (f32[128,256]{1,0:T(8,128)}, f32[128,256]{1,0:T(8,128)S(1)}, u32[]{:S(2)}) copy-start(f32[128,256]{1,0:T(8,128)S(1)} %fusion.45) | copy-start | bytes 393220
  362.2 4.2 collective-permute-start.26
  366.5 4.4 collective-permute-start.27
  368.3 3.3 copy-start.6
  371.6 3.6 collective-permute-start.28
  372.6 9.5 %copy-start.1 = (bf16[768,2048]{1,0:T(8,128)(2,1)S(1)}, bf16[768,2048]{1,0:T(8,128)(2,1)}, u32[]{:S(2)}) copy-start(bf16[768,2048]{1,0:T(8,128)(2,1)} %param.7) | copy-start | bytes 9437188
  376.2 4.3 collective-permute-start.29
  380.5 8.8 %collective-permute-start.30 = (bf16[64,2560]{1,0:T(8,128)(2,1)S(1)}, bf16[64,2560]{1,0:T(8,128)(2,1)S(1)}, u32[]{:S(2)}, u32[]{:S(2)}) collective-permute-start(bf16[64,2560]{1,0:T(8,128)(2,1)S(1)} %maximum_select_fusion.5), channel_id=1, source_target_pairs={{0,4},{1,5},{2,6},{3,7},{4,0},{5,1},{6,2},{7,3},{8,12},{9,13},{10,... | collective-permute-start | bytes 983048 | tf_op jit(solution)/shard_map/ppermute | solution.py:49
  389.5 17.3 %copy-start.14 = (f32[768]{0:T(1024)S(1)}, f32[768]{0:T(1024)}, u32[]{:S(2)}) copy-start(f32[768]{0:T(1024)} %exponential_reduce_fusion) | copy-start | bytes 9220
  389.5 17.9 %collective-permute-start.31 = (bf16[128,2560]{1,0:T(8,128)(2,1)S(1)}, bf16[128,2560]{1,0:T(8,128)(2,1)S(1)}, u32[]{:S(2)}, u32[]{:S(2)}) collective-permute-start(bf16[128,2560]{1,0:T(8,128)(2,1)S(1)} %maximum_select_fusion.3), channel_id=1, source_target_pairs={{0,1},{1,0},{2,3},{3,2},{4,5},{5,4},{6,7},{7,6},{8,9},{9,8},{10,11... | collective-permute-start | bytes 1966088 | tf_op jit(solution)/shard_map/ppermute | solution.py:49
  409.0 2.2 copy-start.5
  411.8 37.2 %copy-start.18 = (s32[2,2]{1,0:T(2,128)S(1)}, s32[2,2]{1,0:T(2,128)}, u32[]{:S(2)}) copy-start(s32[2,2]{1,0:T(2,128)} %copy-done.17) | copy-start | bytes 52
  (6 other events, 8.1 us)
